TPU v7x, 32 devices: a whole 2x2x4 slice. The times are simulated.
32 devices in a mesh: replica: 4 (over y, core), fsdp: 2 (over x), tensor: 4 (over z).
Axes of the slice: x: 2, y: 2, z: 4, core: 2. Of those that a mesh axis runs over, the one named last changes fastest.
Arguments:
- grad_parts: bfloat16 [4, 2, 512, 8192], P('replica', 'fsdp', 'tensor'), may hold values from -12 to 12
- inner_params: float32 [4, 512, 8192], P('replica', 'tensor', 'fsdp'), may hold values from -0.12 to 0.12
- first_moment: float32 [4, 512, 8192], P('replica', 'tensor', 'fsdp'), may hold values from -4 to 4
- second_moment: float32 [4, 512, 8192], P('replica', 'tensor', 'fsdp'), may hold values from 0.1 to 10
- outer_params: float32 [4, 512, 2048], P('replica', 'tensor', 'fsdp'), may hold values from -0.12 to 0.12
- outer_momentum: float32 [4, 512, 2048], P('replica', 'tensor', 'fsdp'), may hold values from -0.06 to 0.06
Outputs:
- next_weights: float32 [512, 8192], P('tensor')
- outer_params_out: float32 [4, 512, 2048], P('replica', 'tensor', 'fsdp')
- outer_momentum_out: float32 [4, 512, 2048], P('replica', 'tensor', 'fsdp')
- first_out: float32 [4, 512, 8192], P('replica', 'tensor', 'fsdp')
- second_out: float32 [4, 512, 8192], P('replica', 'tensor', 'fsdp')
All inputs are finite; a program needn't handle non-finite values.
Results may differ from a plain program's by a relative error of at most 0.0003.
Values may be sent and summed in bfloat16 or wider, within the bound.
No kernel may reach another device: no remote copies, remote signals or barrier semaphores. Data moves between devices by JAX's collectives and lax.ppermute only.
A program may use at most 64 MiB of HBM per device.

v0:
```python
import jax
import jax.numpy as jnp
from jax import lax
from jax.sharding import PartitionSpec as P

STEP = 100


beta_first = 0.9
beta_second = 0.95
inner_rate = 0.01
weight_decay = 0.1
epsilon = 1e-08
outer_rate = 0.7
momentum_factor = 0.9


def inner_adamw(gradient, params, first_in, second_in):
    first_out = beta_first * first_in + (1.0 - beta_first) * gradient
    second_out = beta_second * second_in + (1.0 - beta_second) * gradient * gradient
    first_scale = 1.0 / (1.0 - beta_first**STEP)
    second_scale = 1.0 / (1.0 - beta_second**STEP)
    direction = first_out * first_scale / (jnp.sqrt(second_out * second_scale) + epsilon)
    updated = params - inner_rate * (direction + weight_decay * params)
    return (first_out, second_out, updated)


def nesterov(mean_params, outer_in, momentum):
    pseudo_grad = outer_in - mean_params
    momentum_new = momentum_factor * momentum + pseudo_grad
    params_new = outer_in - outer_rate * (pseudo_grad + momentum_factor * momentum_new)
    return (params_new, momentum_new)


def local(grad_parts, inner_params, first_moment, second_moment, outer_params, outer_momentum):
    replicas = lax.axis_size("replica")
    gradient = lax.psum_scatter(
        grad_parts[0, 0].astype(jnp.float32), "fsdp", scatter_dimension=1, tiled=True
    )
    first_out, second_out, updated = inner_adamw(
        gradient, inner_params[0], first_moment[0], second_moment[0]
    )
    share_cols = outer_params.shape[2]
    totals = lax.psum_scatter(updated, "replica", scatter_dimension=1, tiled=True)
    params_new, momentum_new = nesterov(totals / replicas, outer_params[0], outer_momentum[0])
    pieces = lax.all_gather(params_new[None], ("replica", "fsdp"), axis=0, tiled=True)
    fsdp_count = lax.axis_size("fsdp")
    row_count = params_new.shape[0]
    arranged = pieces.reshape(replicas, fsdp_count, row_count, share_cols).transpose(2, 1, 0, 3)
    next_weights = arranged.reshape(row_count, fsdp_count * replicas * share_cols)
    return (next_weights, params_new[None], momentum_new[None], first_out[None], second_out[None])


def solution(mesh):
    return jax.shard_map(
        local,
        mesh=mesh,
        in_specs=(
            P("replica", "fsdp", "tensor", None),
            P("replica", "tensor", "fsdp"),
            P("replica", "tensor", "fsdp"),
            P("replica", "tensor", "fsdp"),
            P("replica", "tensor", "fsdp"),
            P("replica", "tensor", "fsdp"),
        ),
        out_specs=(
            P("tensor", None),
            P("replica", "tensor", "fsdp"),
            P("replica", "tensor", "fsdp"),
            P("replica", "tensor", "fsdp"),
            P("replica", "tensor", "fsdp"),
        ),
        check_vma=False,
    )
```

profile of v0, /device:TPU:0, one launch (start us, length us, event | category | flops | bytes accessed | tf_op | source)
XLA Modules:
  0.0 165.5 jit_solution(11605220158875495596)
XLA Ops:
  7.2 0.0 reduce-scatter.3.cloned.1.call-start
  7.2 4.0 %bitcast_convert_fusion = f32[128,8192]{1,0:T(8,128)} fusion(bf16[1,1,128,8192]{3,2,1,0:T(8,128)(2,1)} %param.6), kind=kLoop, calls=%fused_computation.2 | loop fusion | flops 1048576 | bytes 6291456 | tf_op jit(solution)/shard_map/convert_element_type | solution.py:38
  11.2 0.0 copy-start
  11.2 0.0 reduce-scatter.3.cloned.1.call-update
  11.3 0.0 reduce-scatter.5.cloned.1.call-start
  11.3 57.2 %reduce-scatter.3.cloned.1.call-done = f32[128,4096]{1,0:T(8,128)} async-done(((f32[128,8192]{1,0:T(8,128)}), f32[128,4096]{1,0:T(8,128)}) %reduce-scatter.3.cloned.1.call-update) | async-done | bytes 2097168 | tf_op jit(solution)/shard_map/reduce_scatter | solution.py:37
  68.5 0.0 copy-done
  68.5 7.1 %fusion.4 = (f32[1,128,4096]{2,1,0:T(8,128)}, f32[128,4096]{1,0:T(8,128)}, f32[1,128,4096]{2,1,0:T(8,128)}) fusion(f32[128,4096]{1,0:T(8,128)} %reduce-scatter.3.cloned.1.call-done, f32[1,128,4096]{2,1,0:T(8,128)S(1)} %copy-done, f32[1,128,4096]{2,1,0:T(8,128)} %param.8, f32[1,128,4096]{2,1,0:T(8,128)} %param.7), kind=kLoop, calls=%fused_computation.9 | loop fusion | flops 7864320 | bytes 14680064 | tf_op jit(solution)/shard_map/broadcast_in_dim | solution.py:51
  75.6 0.0 copy-start.1
  75.7 0.0 copy-start.2
  75.7 0.0 reduce-scatter.5.cloned.1.call-update
  75.7 0.0 all-gather.3.cloned.1.call-start
  75.7 31.3 %reduce-scatter.5.cloned.1.call-done = f32[128,1024]{1,0:T(8,128)} async-done(((f32[128,4096]{1,0:T(8,128)}), f32[128,1024]{1,0:T(8,128)}) %reduce-scatter.5.cloned.1.call-update) | async-done | bytes 524304 | tf_op jit(solution)/shard_map/reduce_scatter | solution.py:44
  107.0 0.0 copy-done.1
  107.0 0.0 copy-done.2
  107.0 2.2 %fusion.5 = (f32[1,128,1024]{2,1,0:T(8,128)}, f32[128,1024]{1,0:T(8,128)}) fusion(f32[128,1024]{1,0:T(8,128)} %reduce-scatter.5.cloned.1.call-done, f32[1,128,1024]{2,1,0:T(8,128)S(1)} %copy-done.1, f32[1,128,1024]{2,1,0:T(8,128)S(1)} %copy-done.2), kind=kLoop, calls=%fused_computation.13 | loop fusion | flops 1048576 | bytes 2621440 | tf_op jit(solution)/shard_map/broadcast_in_dim | solution.py:51
  109.2 0.0 all-gather.3.cloned.1.call-update
  109.2 36.9 %all-gather.3.cloned.1.call-done = f32[1024,1024]{1,0:T(8,128)} async-done(((f32[128,1024]{1,0:T(8,128)}), f32[1024,1024]{1,0:T(8,128)}) %all-gather.3.cloned.1.call-update) | async-done | bytes 4194320 | tf_op jit(solution)/shard_map/all_gather | solution.py:46
  146.1 6.9 %copy.11 = f32[128,2,4,1024]{3,2,1,0:T(4,128)} copy(f32[128,2,4,1024]{3,0,1,2:T(8,128)} %bitcast.51) | data formatting | bytes 8388608 | tf_op jit(solution)/shard_map/transpose | solution.py:49
  153.0 6.0 %reshape.25 = f32[128,8192]{1,0:T(8,128)} reshape(f32[128,2,4,1024]{3,2,1,0:T(4,128)} %copy.11) | data formatting | bytes 8388608 | tf_op jit(solution)/shard_map/reshape | solution.py:50
Async XLA Ops:
  7.2 61.4 %reduce-scatter.3.cloned.1.call-start = ((), (), s32[]{:S(2)}) async-start(), calls=%async_computation.2 | async-start | bytes 6291456 | tf_op jit(solution)/shard_map/reduce_scatter | solution.py:37
  11.2 57.3 %copy-start = (f32[1,128,4096]{2,1,0:T(8,128)S(1)}, f32[1,128,4096]{2,1,0:T(8,128)}, u32[]{:S(2)}) copy-start(f32[1,128,4096]{2,1,0:T(8,128)} %param.9) | copy-start | bytes 6291460
  11.3 95.8 %reduce-scatter.5.cloned.1.call-start = ((), (), s32[]{:S(2)}) async-start(), calls=%async_computation.3 | async-start | bytes 2621440 | tf_op jit(solution)/shard_map/reduce_scatter | solution.py:44
  75.6 31.4 %copy-start.1 = (f32[1,128,1024]{2,1,0:T(8,128)S(1)}, f32[1,128,1024]{2,1,0:T(8,128)}, u32[]{:S(2)}) copy-start(f32[1,128,1024]{2,1,0:T(8,128)} %param.10) | copy-start | bytes 1572868
  75.7 31.4 %copy-start.2 = (f32[1,128,1024]{2,1,0:T(8,128)S(1)}, f32[1,128,1024]{2,1,0:T(8,128)}, u32[]{:S(2)}) copy-start(f32[1,128,1024]{2,1,0:T(8,128)} %param.11) | copy-start | bytes 1572868
  75.7 70.4 %all-gather.3.cloned.1.call-start = ((), (), s32[]{:S(2)}) async-start(), calls=%async_computation.4 | async-start | bytes 4718592 | tf_op jit(solution)/shard_map/all_gather | solution.py:46
Sparse Core Ops, SparseCore 0:
  11.4 57.0 reduce-scatter.2
  75.8 31.1 reduce-scatter.4
  109.5 36.5 all-gather.2
where the time goes:
time: 166 us
  waiting for transfers between devices  125 us (75%)
  between operations  13.7 us (8%)
  other arithmetic  13.3 us (8%)
  local copies, waits for them, and re-layouts  12.9 us (8%)
    reduce_scatter x1, waiting for transfers between devices, local(): lax.psum_scatter(grad_parts[0, 0].astype(jnp.float32), 'fsdp', scatter_di...  57.2 us
    all_gather x1, waiting for transfers between devices, local(): lax.all_gather(params_new[None], ('replica', 'fsdp'), axis=0, tiled=True)  36.9 us
    reduce_scatter x1, waiting for transfers between devices, local(): lax.psum_scatter(updated, 'replica', scatter_dimension=1, tiled=True)  31.3 us
    broadcast_in_dim x1, other arithmetic, local(): second_out[None]  7.13 us
    transpose x1, local copies, waits for them, and re-layouts, local(): pieces.reshape(replicas, fsdp_count, row_count, share_cols)  6.86 us
    reshape x1, local copies, waits for them, and re-layouts, local(): arranged.reshape(row_count, fsdp_count * replicas * share_cols)  6.05 us
    convert_element_type x1, other arithmetic, local(): grad_parts[0, 0].astype(jnp.float32)  4.03 us
  transfers between devices with their start and end apart: 3, of which 3 were waited for; matrix products, arithmetic and copies ran while one was open for 0% of the time, Pallas kernels for 0%

commit v1 on v0

--- a/solution.py
+++ b/solution.py
@@ -32,22 +32,94 @@
     return (params_new, momentum_new)
 
 
+def shifted(count, step, stride=1, offset=None):
+    pairs = []
+    for i in range(count):
+        group, lane = divmod(i, stride)
+        pairs.append((i, ((group + step) % (count // stride)) * stride + lane))
+    return pairs
+
+
+def partner(count):
+    return [(i, i ^ 1) for i in range(count)]
+
+
+def columns(value, index, width):
+    return lax.dynamic_slice_in_dim(value, index * width, width, axis=1)
+
+
+def fsdp_sum(partial):
+    fsdp_count = lax.axis_size("fsdp")
+    me = lax.axis_index("fsdp")
+    cols = partial.shape[1] // fsdp_count
+    gradient = columns(partial, me, cols).astype(jnp.float32)
+    for step in range(1, fsdp_count):
+        send = columns(partial, (me + step) % fsdp_count, cols)
+        got = lax.ppermute(send, "fsdp", shifted(fsdp_count, step))
+        gradient = gradient + got.astype(jnp.float32)
+    return gradient
+
+
+def replica_sum(updated, share_cols):
+    replicas = lax.axis_size("replica")
+    pairs = replicas // 2
+    me = lax.axis_index("replica")
+    core, pair = me % 2, me // 2
+    keep = jnp.concatenate([columns(updated, 2 * q + core, share_cols) for q in range(pairs)], axis=1)
+    send = jnp.concatenate([columns(updated, 2 * q + 1 - core, share_cols) for q in range(pairs)], axis=1)
+    part = keep + lax.ppermute(send, "replica", partner(replicas))
+    total = columns(part, pair, share_cols)
+    for step in range(1, pairs):
+        send = columns(part, (pair + step) % pairs, share_cols)
+        total = total + lax.ppermute(send, "replica", shifted(replicas, step, stride=2))
+    return total
+
+
+def gather_weights(share):
+    replicas = lax.axis_size("replica")
+    fsdp_count = lax.axis_size("fsdp")
+    pairs = replicas // 2
+    me = lax.axis_index("replica")
+    core, pair = me % 2, me // 2
+    f_me = lax.axis_index("fsdp")
+    row_count, share_cols = share.shape
+    out = jnp.zeros((row_count, fsdp_count * replicas * share_cols), share.dtype)
+
+    def put(buf, value, f, q, c):
+        return lax.dynamic_update_slice_in_dim(buf, value, ((f * pairs + q) * 2 + c) * share_cols, axis=1)
+
+    out = put(out, share, f_me, pair, core)
+    out = put(out, lax.ppermute(share, "replica", partner(replicas)), f_me, pair, 1 - core)
+    held = [(share, f_me)]
+    for step in range(1, fsdp_count):
+        got = lax.ppermute(share, "fsdp", shifted(fsdp_count, step))
+        f_src = (f_me + fsdp_count - step) % fsdp_count
+        out = put(out, got, f_src, pair, core)
+        held.append((got, f_src))
+    for got, f_src in held[1:]:
+        out = put(out, lax.ppermute(got, "replica", partner(replicas)), f_src, pair, 1 - core)
+    stacked = jnp.concatenate([value for value, _ in held], axis=1)
+    sources = [f_src for _, f_src in held]
+    for step in range(1, pairs):
+        got = lax.ppermute(stacked, "replica", shifted(replicas, step, stride=2))
+        q_src = (pair + pairs - step) % pairs
+        twin = lax.ppermute(got, "replica", partner(replicas))
+        for index, f_src in enumerate(sources):
+            out = put(out, columns(got, index, share_cols), f_src, q_src, core)
+            out = put(out, columns(twin, index, share_cols), f_src, q_src, 1 - core)
+    return out
+
+
 def local(grad_parts, inner_params, first_moment, second_moment, outer_params, outer_momentum):
     replicas = lax.axis_size("replica")
-    gradient = lax.psum_scatter(
-        grad_parts[0, 0].astype(jnp.float32), "fsdp", scatter_dimension=1, tiled=True
-    )
+    gradient = fsdp_sum(grad_parts[0, 0])
     first_out, second_out, updated = inner_adamw(
         gradient, inner_params[0], first_moment[0], second_moment[0]
     )
     share_cols = outer_params.shape[2]
-    totals = lax.psum_scatter(updated, "replica", scatter_dimension=1, tiled=True)
+    totals = replica_sum(updated, share_cols)
     params_new, momentum_new = nesterov(totals / replicas, outer_params[0], outer_momentum[0])
-    pieces = lax.all_gather(params_new[None], ("replica", "fsdp"), axis=0, tiled=True)
-    fsdp_count = lax.axis_size("fsdp")
-    row_count = params_new.shape[0]
-    arranged = pieces.reshape(replicas, fsdp_count, row_count, share_cols).transpose(2, 1, 0, 3)
-    next_weights = arranged.reshape(row_count, fsdp_count * replicas * share_cols)
+    next_weights = gather_weights(params_new)
     return (next_weights, params_new[None], momentum_new[None], first_out[None], second_out[None])
 
 

time: 166 us -> 104 us (0.63)
  waiting for transfers between devices: 125 us -> 72.7 us
  between operations: 13.7 us -> 0.76 us
  starting transfers between devices: 0.12 us -> 8.88 us
  other arithmetic: 13.3 us -> 8.15 us
    reduce_scatter x2 -> x0, waiting for transfers between devices: 88.5 us -> none  [the longest x1 57.2 us: local(): lax.psum_scatter(grad_parts[0, 0].astype(jnp.float32), 'fsdp', scatter_di...]
    ppermute x0 -> x8, waiting for transfers between devices: none -> 72.7 us  [the longest x1 23.4 us: fsdp_sum(): got = lax.ppermute(send, 'fsdp', shifted(fsdp_count, step))]
    all_gather x1 -> x0, waiting for transfers between devices: 36.9 us -> none  [local(): lax.all_gather(params_new[None], ('replica', 'fsdp'), axis=0, tiled=True)]
    ppermute x0 -> x8, starting transfers between devices: none -> 8.88 us  [the longest x1 2.97 us: fsdp_sum(): got = lax.ppermute(send, 'fsdp', shifted(fsdp_count, step))]
    dynamic_update_slice x0 -> x7, local copies, waits for them, and re-layouts: none -> 7.91 us  [put(): lax.dynamic_update_slice_in_dim(buf, value, ((f * pairs + q) * 2 + c) * s...]
    transpose x1 -> x0, local copies, waits for them, and re-layouts: 6.86 us -> none  [local(): pieces.reshape(replicas, fsdp_count, row_count, share_cols)]
    reshape x1 -> x0, local copies, waits for them, and re-layouts: 6.05 us -> none  [local(): arranged.reshape(row_count, fsdp_count * replicas * share_cols)]
    convert_element_type x1 -> x0, other arithmetic: 4.03 us -> none  [local(): grad_parts[0, 0].astype(jnp.float32)]
  transfers between devices with their start and end apart: 3 -> 8, of which waited for: 3 -> 6; matrix products, arithmetic and copies ran while one was open for 0% -> 3% of each run, Pallas kernels for 0% -> 0%
where the time goes in v1:
time: 104 us; the launch traced here: 103 us
  waiting for transfers between devices  72.7 us (70%)
  local copies, waits for them, and re-layouts  13 us (12%)
  starting transfers between devices  8.88 us (9%)
  other arithmetic  8.15 us (8%)
    ppermute x1, waiting for transfers between devices, fsdp_sum(): got = lax.ppermute(send, 'fsdp', shifted(fsdp_count, step))  23.4 us
    ppermute x1, waiting for transfers between devices, gather_weights(): got = lax.ppermute(stacked, 'replica', shifted(replicas, step, stride=2))  21.8 us
    ppermute x1, waiting for transfers between devices, replica_sum(): lax.ppermute(send, 'replica', shifted(replicas, step, stride=2))  12.2 us
    ppermute x1, waiting for transfers between devices, gather_weights(): got = lax.ppermute(share, 'fsdp', shifted(fsdp_count, step))  11.4 us
    dynamic_update_slice x7, local copies, waits for them, and re-layouts, put(): lax.dynamic_update_slice_in_dim(buf, value, ((f * pairs + q) * 2 + c) * s...  7.91 us
    broadcast_in_dim x1, other arithmetic, local(): second_out[None]  6.63 us
    ppermute x1, starting transfers between devices, fsdp_sum(): got = lax.ppermute(send, 'fsdp', shifted(fsdp_count, step))  2.97 us
    dynamic_slice x3, local copies, waits for them, and re-layouts, columns(): return lax.dynamic_slice_in_dim(value, index * width, width, axis=1)  2.64 us
  transfers between devices with their start and end apart: 8, of which 6 were waited for; matrix products, arithmetic and copies ran while one was open for 3% of the time, Pallas kernels for 0%

profile of v1, /device:TPU:0, one launch (start us, length us, event | category | flops | bytes accessed | tf_op | source)
XLA Modules:
  0.0 103.5 jit_solution(2208875818283605073)
XLA Ops:
  0.7 2.4 %dynamic-slice_bitcast_fusion = bf16[128,4096]{1,0:T(8,128)(2,1)} fusion(bf16[1,1,128,8192]{3,2,1,0:T(8,128)(2,1)} %param.6, s32[]{:T(128)S(6)} %select_n.76), kind=kLoop, calls=%fused_computation.11 | loop fusion | bytes 2097156 | tf_op jit(solution)/shard_map/dynamic_slice | solution.py:48
  3.1 3.0 %collective-permute-start = (bf16[128,4096]{1,0:T(8,128)(2,1)}, bf16[128,4096]{1,0:T(8,128)(2,1)S(1)}, u32[]{:S(2)}, u32[]{:S(2)}) collective-permute-start(bf16[128,4096]{1,0:T(8,128)(2,1)} %dynamic-slice_bitcast_fusion), channel_id=1, source_target_pairs={{0,4},{4,0},{1,5},{5,1},{2,6},{6,2},{3,7},{7,3},{8,12},{12,8},{9,1... | collective-permute-start | bytes 3145736 | tf_op jit(solution)/shard_map/ppermute | solution.py:58
  6.1 23.4 %collective-permute-done = bf16[128,4096]{1,0:T(8,128)(2,1)S(1)} collective-permute-done((bf16[128,4096]{1,0:T(8,128)(2,1)}, bf16[128,4096]{1,0:T(8,128)(2,1)S(1)}, u32[]{:S(2)}, u32[]{:S(2)}) %collective-permute-start) | collective-permute-done | bytes 1048608 | tf_op jit(solution)/shard_map/ppermute | solution.py:58
  29.4 6.6 %fusion.5 = (f32[1,128,4096]{2,1,0:T(8,128)}, f32[128,4096]{1,0:T(8,128)S(1)}, f32[1,128,4096]{2,1,0:T(8,128)}) fusion(bf16[128,4096]{1,0:T(8,128)(2,1)S(1)} %collective-permute-done, bf16[1,1,128,8192]{3,2,1,0:T(8,128)(2,1)S(1)} %copy-done, s32[]{:T(128)S(6)} %select_n.74, f32[1,128,4096]{2,1,0:T(8,128)} %param.9, f32[1,128,4096]{2,1,0:T(8,128)} %param.8, ...), kind=kLoop, calls=%fused_computation.21 | loop fusion | flops 9437184 | bytes 14680068 | tf_op jit(solution)/shard_map/broadcast_in_dim | solution.py:123
  36.1 0.2 constant_dynamic-slice_fusion.4
  36.4 2.6 %collective-permute-done.1 = f32[128,2048]{1,0:T(8,128)S(1)} collective-permute-done((f32[128,2048]{1,0:T(8,128)S(1)}, f32[128,2048]{1,0:T(8,128)S(1)}, u32[]{:S(2)}, u32[]{:S(2)}) %collective-permute-start.1) | collective-permute-done | bytes 1048608 | tf_op jit(solution)/shard_map/ppermute | solution.py:70
  39.0 0.1 maximum_add_fusion
  39.2 1.8 %collective-permute-start.2 = (f32[128,1024]{1,0:T(8,128)S(1)}, f32[128,1024]{1,0:T(8,128)S(1)}, u32[]{:S(2)}, u32[]{:S(2)}) collective-permute-start(f32[128,1024]{1,0:T(8,128)S(1)} %constant_dynamic-slice_fusion), channel_id=1, source_target_pairs={{0,16},{8,24},{16,0},{24,8},{1,17},{9,25},{17,1},{25,9},{2,18},{10... | collective-permute-start | bytes 1572872 | tf_op jit(solution)/shard_map/ppermute | solution.py:74
  41.1 12.2 %collective-permute-done.2 = f32[128,1024]{1,0:T(8,128)S(1)} collective-permute-done((f32[128,1024]{1,0:T(8,128)S(1)}, f32[128,1024]{1,0:T(8,128)S(1)}, u32[]{:S(2)}, u32[]{:S(2)}) %collective-permute-start.2) | collective-permute-done | bytes 524320 | tf_op jit(solution)/shard_map/ppermute | solution.py:74
  53.3 2.5 %broadcast_in_dim.15 = f32[128,8192]{1,0:T(8,128)} broadcast(f32[]{:T(128)} %constant.73.clone.1), dimensions={} | broadcast | bytes 4194308 | tf_op jit(solution)/shard_map/broadcast_in_dim | solution.py:86
  55.8 1.2 %constant_dynamic-update-slice_fusion.3 = (f32[128,8192]{1,0:T(8,128)}, f32[128,1024]{1,0:T(8,128)S(1)}, f32[1,128,1024]{2,1,0:T(8,128)}) fusion(f32[128,8192]{1,0:T(8,128)} %broadcast_in_dim.15, s32[]{:T(128)S(6)} %select_n.86, f32[1,128,1024]{2,1,0:T(8,128)S(1)} %copy-done.2, f32[128,1024]{1,0:T(8,128)S(1)} %collective-permute-done.2, ...), kind=kLoop, calls=%fused_computation.25 | loop fusion | flops 1179648 | bytes 3670024 | tf_op jit(solution)/shard_map/dynamic_update_slice | solution.py:89
  57.0 1.7 %collective-permute-start.4 = (f32[128,1024]{1,0:T(8,128)S(1)}, f32[128,1024]{1,0:T(8,128)S(1)}, u32[]{:S(2)}, u32[]{:S(2)}) collective-permute-start(f32[128,1024]{1,0:T(8,128)S(1)} %get-tuple-element.6), channel_id=1, source_target_pairs={{0,4},{4,0},{1,5},{5,1},{2,6},{6,2},{3,7},{7,3},{8,12},{12,8},{9,1... | collective-permute-start | bytes 1572872 | tf_op jit(solution)/shard_map/ppermute | solution.py:95
  58.7 11.4 %collective-permute-done.4 = f32[128,1024]{1,0:T(8,128)S(1)} collective-permute-done((f32[128,1024]{1,0:T(8,128)S(1)}, f32[128,1024]{1,0:T(8,128)S(1)}, u32[]{:S(2)}, u32[]{:S(2)}) %collective-permute-start.4) | collective-permute-done | bytes 524320 | tf_op jit(solution)/shard_map/ppermute | solution.py:95
  70.2 1.8 %collective-permute-start.6 = (f32[128,2048]{1,0:T(8,128)S(1)}, f32[128,2048]{1,0:T(8,128)S(1)}, u32[]{:S(2)}, u32[]{:S(2)}) collective-permute-start(f32[128,2048]{1,0:T(8,128)S(1)} %pad_maximum_fusion.1), channel_id=1, source_target_pairs={{0,16},{8,24},{16,0},{24,8},{1,17},{9,25},{17,1},{25,9},{2,18},{10... | collective-permute-start | bytes 3145736 | tf_op jit(solution)/shard_map/ppermute | solution.py:104
  72.0 21.8 %collective-permute-done.6 = f32[128,2048]{1,0:T(8,128)S(1)} collective-permute-done((f32[128,2048]{1,0:T(8,128)S(1)}, f32[128,2048]{1,0:T(8,128)S(1)}, u32[]{:S(2)}, u32[]{:S(2)}) %collective-permute-start.6) | collective-permute-done | bytes 1048608 | tf_op jit(solution)/shard_map/ppermute | solution.py:104
  93.8 0.5 collective-permute-start.5
  94.3 0.8 constant_dynamic-update-slice_fusion.2
  95.1 0.8 constant_dynamic-update-slice_fusion.1
  96.0 1.2 %collective-permute-done.5 = f32[128,1024]{1,0:T(8,128)S(1)} collective-permute-done((f32[128,1024]{1,0:T(8,128)S(1)}, f32[128,1024]{1,0:T(8,128)S(1)}, u32[]{:S(2)}, u32[]{:S(2)}) %collective-permute-start.5) | collective-permute-done | bytes 524320 | tf_op jit(solution)/shard_map/ppermute | solution.py:100
  97.2 0.8 constant_dynamic-update-slice_fusion
  98.0 0.8 slice_dynamic-update-slice_fusion.3
  98.9 1.9 %slice_dynamic-update-slice_fusion.2 = f32[128,8192]{1,0:T(8,128)} fusion(f32[128,8192]{1,0:T(8,128)} %slice_dynamic-update-slice_fusion.3, s32[]{:T(128)S(6)} %select_n.91, f32[128,2048]{1,0:T(8,128)} %collective-permute-done.7), kind=kLoop, calls=%fused_computation.14 | loop fusion | bytes 1048580 | tf_op jit(solution)/shard_map/dynamic_update_slice | solution.py:89
  100.8 0.8 slice_dynamic-update-slice_fusion.1
  101.6 1.9 %slice_dynamic-update-slice_fusion = f32[128,8192]{1,0:T(8,128)} fusion(f32[128,8192]{1,0:T(8,128)} %slice_dynamic-update-slice_fusion.1, s32[]{:T(128)S(6)} %select_n.93, f32[128,2048]{1,0:T(8,128)} %collective-permute-done.7), kind=kLoop, calls=%fused_computation.12 | loop fusion | bytes 1048580 | tf_op jit(solution)/shard_map/dynamic_update_slice | solution.py:89
  (16 shorter events, 0.3 us)
Async XLA Ops:
  0.6 28.8 %copy-start = (bf16[1,1,128,8192]{3,2,1,0:T(8,128)(2,1)S(1)}, bf16[1,1,128,8192]{3,2,1,0:T(8,128)(2,1)}, u32[]{:S(2)}) copy-start(bf16[1,1,128,8192]{3,2,1,0:T(8,128)(2,1)} %param.6) | copy-start | bytes 6291460
  3.1 26.3 %collective-permute-start = (bf16[128,4096]{1,0:T(8,128)(2,1)}, bf16[128,4096]{1,0:T(8,128)(2,1)S(1)}, u32[]{:S(2)}, u32[]{:S(2)}) collective-permute-start(bf16[128,4096]{1,0:T(8,128)(2,1)} %dynamic-slice_bitcast_fusion), channel_id=1, source_target_pairs={{0,4},{4,0},{1,5},{5,1},{2,6},{6,2},{3,7},{7,3},{8,12},{12,8},{9,1... | collective-permute-start | bytes 3145736 | tf_op jit(solution)/shard_map/ppermute | solution.py:58
  36.3 2.7 %collective-permute-start.1 = (f32[128,2048]{1,0:T(8,128)S(1)}, f32[128,2048]{1,0:T(8,128)S(1)}, u32[]{:S(2)}, u32[]{:S(2)}) collective-permute-start(f32[128,2048]{1,0:T(8,128)S(1)} %pad_maximum_fusion), channel_id=1, source_target_pairs={{0,8},{8,0},{16,24},{24,16},{1,9},{9,1},{17,25},{25,17},{2,10},{10... | collective-permute-start | bytes 3145736 | tf_op jit(solution)/shard_map/ppermute | solution.py:70
  39.2 14.1 %collective-permute-start.2 = (f32[128,1024]{1,0:T(8,128)S(1)}, f32[128,1024]{1,0:T(8,128)S(1)}, u32[]{:S(2)}, u32[]{:S(2)}) collective-permute-start(f32[128,1024]{1,0:T(8,128)S(1)} %constant_dynamic-slice_fusion), channel_id=1, source_target_pairs={{0,16},{8,24},{16,0},{24,8},{1,17},{9,25},{17,1},{25,9},{2,18},{10... | collective-permute-start | bytes 1572872 | tf_op jit(solution)/shard_map/ppermute | solution.py:74
  41.1 14.7 %copy-start.2 = (f32[1,128,1024]{2,1,0:T(8,128)S(1)}, f32[1,128,1024]{2,1,0:T(8,128)}, u32[]{:S(2)}) copy-start(f32[1,128,1024]{2,1,0:T(8,128)} %param.11) | copy-start | bytes 1572868
  41.1 14.7 %copy-start.3 = (f32[1,128,1024]{2,1,0:T(8,128)S(1)}, f32[1,128,1024]{2,1,0:T(8,128)}, u32[]{:S(2)}) copy-start(f32[1,128,1024]{2,1,0:T(8,128)} %param.10) | copy-start | bytes 1572868
  57.0 39.0 %copy-start.1 = (f32[128,1024]{1,0:T(8,128)}, f32[128,1024]{1,0:T(8,128)S(1)}, u32[]{:S(2)}) copy-start(f32[128,1024]{1,0:T(8,128)S(1)} %get-tuple-element.6) | copy-start | bytes 1572868
  57.0 13.1 %collective-permute-start.4 = (f32[128,1024]{1,0:T(8,128)S(1)}, f32[128,1024]{1,0:T(8,128)S(1)}, u32[]{:S(2)}, u32[]{:S(2)}) collective-permute-start(f32[128,1024]{1,0:T(8,128)S(1)} %get-tuple-element.6), channel_id=1, source_target_pairs={{0,4},{4,0},{1,5},{5,1},{2,6},{6,2},{3,7},{7,3},{8,12},{12,8},{9,1... | collective-permute-start | bytes 1572872 | tf_op jit(solution)/shard_map/ppermute | solution.py:95
  70.2 23.6 %collective-permute-start.6 = (f32[128,2048]{1,0:T(8,128)S(1)}, f32[128,2048]{1,0:T(8,128)S(1)}, u32[]{:S(2)}, u32[]{:S(2)}) collective-permute-start(f32[128,2048]{1,0:T(8,128)S(1)} %pad_maximum_fusion.1), channel_id=1, source_target_pairs={{0,16},{8,24},{16,0},{24,8},{1,17},{9,25},{17,1},{25,9},{2,18},{10... | collective-permute-start | bytes 3145736 | tf_op jit(solution)/shard_map/ppermute | solution.py:104
  72.0 22.3 %collective-permute-start.3 = (f32[128,1024]{1,0:T(8,128)S(1)}, f32[128,1024]{1,0:T(8,128)S(1)}, u32[]{:S(2)}, u32[]{:S(2)}) collective-permute-start(f32[128,1024]{1,0:T(8,128)S(1)} %get-tuple-element.6), channel_id=1, source_target_pairs={{0,8},{8,0},{16,24},{24,16},{1,9},{9,1},{17,25},{25,17},{2,10},{10... | collective-permute-start | bytes 1572872 | tf_op jit(solution)/shard_map/ppermute | solution.py:92
  93.8 5.1 %collective-permute-start.7 = (f32[128,2048]{1,0:T(8,128)S(1)}, f32[128,2048]{1,0:T(8,128)}, u32[]{:S(2)}, u32[]{:S(2)}) collective-permute-start(f32[128,2048]{1,0:T(8,128)S(1)} %collective-permute-done.6), channel_id=1, source_target_pairs={{0,8},{8,0},{16,24},{24,16},{1,9},{9,1},{17,25},{25,17},{2,10},{10... | collective-permute-start | bytes 3145736 | tf_op jit(solution)/shard_map/ppermute | solution.py:106
  93.8 3.4 %collective-permute-start.5 = (f32[128,1024]{1,0:T(8,128)S(1)}, f32[128,1024]{1,0:T(8,128)S(1)}, u32[]{:S(2)}, u32[]{:S(2)}) collective-permute-start(f32[128,1024]{1,0:T(8,128)S(1)} %collective-permute-done.4), channel_id=1, source_target_pairs={{0,8},{8,0},{16,24},{24,16},{1,9},{9,1},{17,25},{25,17},{2,10},{10... | collective-permute-start | bytes 1572872 | tf_op jit(solution)/shard_map/ppermute | solution.py:100

commit v2 on v1

--- a/solution.py
+++ b/solution.py
@@ -83,43 +83,61 @@
     core, pair = me % 2, me // 2
     f_me = lax.axis_index("fsdp")
     row_count, share_cols = share.shape
+    pieces = [(share, f_me, pair, core)]
+    pieces.append((lax.ppermute(share, "replica", partner(replicas)), f_me, pair, 1 - core))
+    along_x = {}
+    for step in range(1, fsdp_count):
+        along_x[step] = lax.ppermute(share, "fsdp", shifted(fsdp_count, step))
+    along_y = {}
+    for step in range(1, pairs):
+        along_y[step] = lax.ppermute(share, "replica", shifted(replicas, step, stride=2))
+    held = [(value, (f_me + fsdp_count - step) % fsdp_count, pair) for step, value in along_x.items()]
+    held += [(value, f_me, (pair + pairs - step) % pairs) for step, value in along_y.items()]
+    for step_f in range(1, fsdp_count):
+        for step_q in range(1, pairs):
+            payload = jnp.where(core == 0, along_y[step_q], along_x[step_f])
+            routes = []
+            for r in range(replicas):
+                for f in range(fsdp_count):
+                    q, c = divmod(r, 2)
+                    if c == 0:
+                        routes.append((r * fsdp_count + f, r * fsdp_count + (f + step_f) % fsdp_count))
+                    else:
+                        routes.append((r * fsdp_count + f, (((q + step_q) % pairs) * 2 + c) * fsdp_count + f))
+            got = lax.ppermute(payload, ("replica", "fsdp"), routes)
+            held.append((got, (f_me + fsdp_count - step_f) % fsdp_count, (pair + pairs - step_q) % pairs))
+    stacked = jnp.concatenate([value for value, _, _ in held], axis=1)
+    twin = lax.ppermute(stacked, "replica", partner(replicas))
+    for index, (value, f_src, q_src) in enumerate(held):
+        pieces.append((value, f_src, q_src, core))
+        pieces.append((columns(twin, index, share_cols), f_src, q_src, 1 - core))
     out = jnp.zeros((row_count, fsdp_count * replicas * share_cols), share.dtype)
+    for value, f, q, c in pieces:
+        out = lax.dynamic_update_slice_in_dim(out, value, ((f * pairs + q) * 2 + c) * share_cols, axis=1)
+    return out
 
-    def put(buf, value, f, q, c):
-        return lax.dynamic_update_slice_in_dim(buf, value, ((f * pairs + q) * 2 + c) * share_cols, axis=1)
 
-    out = put(out, share, f_me, pair, core)
-    out = put(out, lax.ppermute(share, "replica", partner(replicas)), f_me, pair, 1 - core)
-    held = [(share, f_me)]
-    for step in range(1, fsdp_count):
-        got = lax.ppermute(share, "fsdp", shifted(fsdp_count, step))
-        f_src = (f_me + fsdp_count - step) % fsdp_count
-        out = put(out, got, f_src, pair, core)
-        held.append((got, f_src))
-    for got, f_src in held[1:]:
-        out = put(out, lax.ppermute(got, "replica", partner(replicas)), f_src, pair, 1 - core)
-    stacked = jnp.concatenate([value for value, _ in held], axis=1)
-    sources = [f_src for _, f_src in held]
-    for step in range(1, pairs):
-        got = lax.ppermute(stacked, "replica", shifted(replicas, step, stride=2))
-        q_src = (pair + pairs - step) % pairs
-        twin = lax.ppermute(got, "replica", partner(replicas))
-        for index, f_src in enumerate(sources):
-            out = put(out, columns(got, index, share_cols), f_src, q_src, core)
-            out = put(out, columns(twin, index, share_cols), f_src, q_src, 1 - core)
-    return out
+CHUNKS = 4
 
 
 def local(grad_parts, inner_params, first_moment, second_moment, outer_params, outer_momentum):
     replicas = lax.axis_size("replica")
-    gradient = fsdp_sum(grad_parts[0, 0])
-    first_out, second_out, updated = inner_adamw(
-        gradient, inner_params[0], first_moment[0], second_moment[0]
-    )
     share_cols = outer_params.shape[2]
-    totals = replica_sum(updated, share_cols)
-    params_new, momentum_new = nesterov(totals / replicas, outer_params[0], outer_momentum[0])
-    next_weights = gather_weights(params_new)
+    row_count = inner_params.shape[1]
+    chunk = row_count // CHUNKS
+    pieces = []
+    for index in range(CHUNKS):
+        rows = slice(index * chunk, (index + 1) * chunk)
+        gradient = fsdp_sum(grad_parts[0, 0, rows])
+        first_out, second_out, updated = inner_adamw(
+            gradient, inner_params[0, rows], first_moment[0, rows], second_moment[0, rows]
+        )
+        totals = replica_sum(updated, share_cols)
+        params_new, momentum_new = nesterov(totals / replicas, outer_params[0, rows], outer_momentum[0, rows])
+        next_weights = gather_weights(params_new)
+        pieces.append((next_weights, params_new, momentum_new, first_out, second_out))
+    outs = [jnp.concatenate(parts, axis=0) for parts in zip(*pieces)]
+    next_weights, params_new, momentum_new, first_out, second_out = outs
     return (next_weights, params_new[None], momentum_new[None], first_out[None], second_out[None])
 
 

time: 104 us -> 80.1 us (0.77)
  waiting for transfers between devices: 72.7 us -> 39.2 us
  starting transfers between devices: 8.88 us -> 23 us
  local copies, waits for them, and re-layouts: 13 us -> 4.1 us
  other arithmetic: 8.15 us -> 12.3 us
    ppermute x4 -> x16, waiting for transfers between devices: 34.5 us -> 12.2 us  [the longest x4 6.42 us: gather_weights(): lax.ppermute(share, 'replica', shifted(replicas, step, stride=2))]
    ppermute x4 -> x16, starting transfers between devices: 4 us -> 12 us  [the longest x4 5.01 us: gather_weights(): along_x[step] = lax.ppermute(share, 'fsdp', shifted(fsdp_count, step))]
    dynamic_update_slice x7 -> x24, local copies, waits for them, and re-layouts: 7.91 us -> 0.38 us  [gather_weights(): lax.dynamic_update_slice_in_dim(out, value, ((f * pairs + q) * 2 + c) * s...]
    ppermute x1 -> x4, waiting for transfers between devices: 23.4 us -> 17.7 us  [fsdp_sum(): got = lax.ppermute(send, 'fsdp', shifted(fsdp_count, step))]
    sub x0 -> x2, other arithmetic: none -> 5.07 us  [inner_adamw(): updated = params - inner_rate * (direction + weight_decay * params)]
    ppermute x1 -> x4, waiting for transfers between devices: 12.2 us -> 9.38 us  [replica_sum(): lax.ppermute(send, 'replica', shifted(replicas, step, stride=2))]
    ppermute x1 -> x4, waiting for transfers between devices: 2.61 us -> 0.01 us  [replica_sum(): part = keep + lax.ppermute(send, 'replica', partner(replicas))]
    broadcast_in_dim x1 -> x3, other arithmetic: 6.63 us -> 4.12 us  [the longest x1 2.46 us: local(): first_out[None]]
  transfers between devices with their start and end apart: 8 -> 32, of which waited for: 6 -> 11; matrix products, arithmetic and copies ran while one was open for 3% -> 11% of each run, Pallas kernels for 0% -> 0%
where the time goes in v2:
time: 80.1 us; the launch traced here: 79.9 us
  waiting for transfers between devices  39.2 us (49%)
  starting transfers between devices  23 us (29%)
  other arithmetic  12.3 us (15%)
  local copies, waits for them, and re-layouts  4.1 us (5%)
  between operations  1.22 us (2%)
    ppermute x4, waiting for transfers between devices, fsdp_sum(): got = lax.ppermute(send, 'fsdp', shifted(fsdp_count, step))  17.7 us
    ppermute x4, waiting for transfers between devices, replica_sum(): lax.ppermute(send, 'replica', shifted(replicas, step, stride=2))  9.38 us
    ppermute x4, waiting for transfers between devices, gather_weights(): lax.ppermute(share, 'replica', shifted(replicas, step, stride=2))  6.42 us
    ppermute x4, starting transfers between devices, fsdp_sum(): got = lax.ppermute(send, 'fsdp', shifted(fsdp_count, step))  5.15 us
    sub x2, other arithmetic, inner_adamw(): updated = params - inner_rate * (direction + weight_decay * params)  5.07 us
    ppermute x4, starting transfers between devices, gather_weights(): along_x[step] = lax.ppermute(share, 'fsdp', shifted(fsdp_count, step))  5.01 us
    ppermute x4, starting transfers between devices, replica_sum(): lax.ppermute(send, 'replica', shifted(replicas, step, stride=2))  4.31 us
    ppermute x4, waiting for transfers between devices, gather_weights(): got = lax.ppermute(payload, ('replica', 'fsdp'), routes)  3.91 us
  transfers between devices with their start and end apart: 32, of which 11 were waited for; matrix products, arithmetic and copies ran while one was open for 11% of the time, Pallas kernels for 0%

profile of v2, /device:TPU:0, one launch (start us, length us, event | category | flops | bytes accessed | tf_op | source)
XLA Modules:
  0.0 79.9 jit_solution(15424965800060901581)
XLA Ops:
  0.6 1.7 %fusion.16 = (bf16[1,1,32,8192]{3,2,1,0:T(8,128)(2,1)S(1)}, bf16[1,1,32,8192]{3,2,1,0:T(8,128)(2,1)S(1)}, bf16[1,1,32,8192]{3,2,1,0:T(8,128)(2,1)S(1)}, bf16[1,1,32,8192]{3,2,1,0:T(8,128)(2,1)S(1)}) fusion(bf16[1,1,128,8192]{3,2,1,0:T(8,128)(2,1)} %param.6), kind=kLoop, calls=%fused_computation.121 | loop fusion | bytes 4194304 | tf_op jit(solution)/shard_map/slice | solution.py:131
  2.3 3.0 %collective-permute-start = (bf16[32,4096]{1,0:T(8,128)(2,1)S(1)}, bf16[32,4096]{1,0:T(8,128)(2,1)S(1)}, u32[]{:S(2)}, u32[]{:S(2)}) collective-permute-start(bf16[32,4096]{1,0:T(8,128)(2,1)S(1)} %dynamic-slice_bitcast_fusion.3), channel_id=1, source_target_pairs={{0,4},{4,0},{1,5},{5,1},{2,6},{6,2},{3,7},{7,3},{8,12},{12,8},{9,1... | collective-permute-start | bytes 786440 | tf_op jit(solution)/shard_map/ppermute | solution.py:58
  6.2 2.0 %collective-permute-start.16 = (bf16[32,4096]{1,0:T(8,128)(2,1)}, bf16[32,4096]{1,0:T(8,128)(2,1)}, u32[]{:S(2)}, u32[]{:S(2)}) collective-permute-start(bf16[32,4096]{1,0:T(8,128)(2,1)} %dynamic-slice_bitcast_fusion.1), channel_id=1, source_target_pairs={{0,4},{4,0},{1,5},{5,1},{2,6},{6,2},{3,7},{7,3},{8,12},{12,8},{9,1... | collective-permute-start | bytes 786440 | tf_op jit(solution)/shard_map/ppermute | solution.py:58
  9.0 14.9 %collective-permute-done.16 = bf16[32,4096]{1,0:T(8,128)(2,1)} collective-permute-done((bf16[32,4096]{1,0:T(8,128)(2,1)}, bf16[32,4096]{1,0:T(8,128)(2,1)}, u32[]{:S(2)}, u32[]{:S(2)}) %collective-permute-start.16) | collective-permute-done | bytes 262176 | tf_op jit(solution)/shard_map/ppermute | solution.py:58
  23.9 1.9 %bitcast_subtract_fusion.1 = (f32[32,4096]{1,0:T(8,128)S(1)}, f32[32,4096]{1,0:T(8,128)S(1)}, f32[32,4096]{1,0:T(8,128)S(1)}) fusion(f32[1,128,4096]{2,1,0:T(8,128)} %param.7, bf16[32,4096]{1,0:T(8,128)(2,1)} %collective-permute-done.16, bf16[1,1,32,8192]{3,2,1,0:T(8,128)(2,1)S(1)} %get-tuple-element.42, s32[]{:T(128)S(6)} %select_n.200, ...), kind=kLoop, calls=%fused_computation.23 | loop fusion | flops 2359296 | bytes 3670020 | tf_op jit(solution)/shard_map/sub | solution.py:24
  25.8 2.7 %collective-permute-done.8 = bf16[32,4096]{1,0:T(8,128)(2,1)S(1)} collective-permute-done((bf16[32,4096]{1,0:T(8,128)(2,1)}, bf16[32,4096]{1,0:T(8,128)(2,1)S(1)}, u32[]{:S(2)}, u32[]{:S(2)}) %collective-permute-start.8) | collective-permute-done | bytes 262176 | tf_op jit(solution)/shard_map/ppermute | solution.py:58
  28.5 3.2 %bitcast_subtract_fusion.3 = (f32[32,4096]{1,0:T(8,128)S(1)}, f32[32,4096]{1,0:T(8,128)S(1)}, f32[32,4096]{1,0:T(8,128)S(1)}, f32[32,4096]{1,0:T(8,128)S(1)}, f3...) fusion(f32[1,128,4096]{2,1,0:T(8,128)S(1)} %copy-done.2, ...), kind=kLoop, calls=%fused_computation.33 | loop fusion | flops 7077888 | bytes 11010052 | tf_op jit(solution)/shard_map/sub | solution.py:24
  33.3 2.5 %maximum_bitcast_fusion = (f32[1,128,4096]{2,1,0:T(8,128)}, f32[1,128,4096]{2,1,0:T(8,128)}) fusion(f32[32,4096]{1,0:T(8,128)S(1)} %get-tuple-element.38, f32[32,4096]{1,0:T(8,128)S(1)} %get-tuple-element.26, f32[32,4096]{1,0:T(8,128)S(1)} %get-tuple-element.35, f32[32,4096]{1,0:T(8,128)S(1)} %get-tuple-element.16, f32[32,4096]{1,0:T(8,128)S(1)} %get-tuple-element.37, ...), kind=kLoop, calls=%fused_computation.1 | loop fusion | flops 3145728 | bytes 8388608 | tf_op jit(solution)/shard_map/broadcast_in_dim | solution.py:141
  35.9 1.8 %collective-permute-start.18 = (f32[32,1024]{1,0:T(8,128)S(1)}, f32[32,1024]{1,0:T(8,128)S(1)}, u32[]{:S(2)}, u32[]{:S(2)}) collective-permute-start(f32[32,1024]{1,0:T(8,128)S(1)} %constant_dynamic-slice_fusion.5), channel_id=1, source_target_pairs={{0,16},{8,24},{16,0},{24,8},{1,17},{9,25},{17,1},{25,9},{2,18},{10... | collective-permute-start | bytes 393224 | tf_op jit(solution)/shard_map/ppermute | solution.py:74
  38.1 1.8 %collective-permute-start.2 = (f32[32,1024]{1,0:T(8,128)S(1)}, f32[32,1024]{1,0:T(8,128)S(1)}, u32[]{:S(2)}, u32[]{:S(2)}) collective-permute-start(f32[32,1024]{1,0:T(8,128)S(1)} %constant_dynamic-slice_fusion.15), channel_id=1, source_target_pairs={{0,16},{8,24},{16,0},{24,8},{1,17},{9,25},{17,1},{25,9},{2,18},{10... | collective-permute-start | bytes 393224 | tf_op jit(solution)/shard_map/ppermute | solution.py:74
  40.4 7.5 %collective-permute-done.2 = f32[32,1024]{1,0:T(8,128)S(1)} collective-permute-done((f32[32,1024]{1,0:T(8,128)S(1)}, f32[32,1024]{1,0:T(8,128)S(1)}, u32[]{:S(2)}, u32[]{:S(2)}) %collective-permute-start.2) | collective-permute-done | bytes 131104 | tf_op jit(solution)/shard_map/ppermute | solution.py:74
  48.0 1.8 %collective-permute-done.10 = f32[32,1024]{1,0:T(8,128)S(1)} collective-permute-done((f32[32,1024]{1,0:T(8,128)S(1)}, f32[32,1024]{1,0:T(8,128)S(1)}, u32[]{:S(2)}, u32[]{:S(2)}) %collective-permute-start.10) | collective-permute-done | bytes 131104 | tf_op jit(solution)/shard_map/ppermute | solution.py:74
  50.2 1.8 %collective-permute-start.4 = (f32[32,1024]{1,0:T(8,128)S(1)}, f32[32,1024]{1,0:T(8,128)S(1)}, u32[]{:S(2)}, u32[]{:S(2)}) collective-permute-start(f32[32,1024]{1,0:T(8,128)S(1)} %get-tuple-element.14), channel_id=1, source_target_pairs={{0,4},{4,0},{1,5},{5,1},{2,6},{6,2},{3,7},{7,3},{8,12},{12,8},{9,1... | collective-permute-start | bytes 393224 | tf_op jit(solution)/shard_map/ppermute | solution.py:90
  51.9 1.5 %collective-permute-start.5 = (f32[32,1024]{1,0:T(8,128)S(1)}, f32[32,1024]{1,0:T(8,128)S(1)}, u32[]{:S(2)}, u32[]{:S(2)}) collective-permute-start(f32[32,1024]{1,0:T(8,128)S(1)} %get-tuple-element.14), channel_id=1, source_target_pairs={{0,16},{8,24},{16,0},{24,8},{1,17},{9,25},{17,1},{25,9},{2,18},{10... | collective-permute-start | bytes 393224 | tf_op jit(solution)/shard_map/ppermute | solution.py:93
  56.6 0.9 %collective-permute-done.5 = f32[32,1024]{1,0:T(8,128)S(1)} collective-permute-done((f32[32,1024]{1,0:T(8,128)S(1)}, f32[32,1024]{1,0:T(8,128)S(1)}, u32[]{:S(2)}, u32[]{:S(2)}) %collective-permute-start.5) | collective-permute-done | bytes 131104 | tf_op jit(solution)/shard_map/ppermute | solution.py:93
  57.5 0.8 %collective-permute-start.20 = (f32[32,1024]{1,0:T(8,128)S(1)}, f32[32,1024]{1,0:T(8,128)S(1)}, u32[]{:S(2)}, u32[]{:S(2)}) collective-permute-start(f32[32,1024]{1,0:T(8,128)S(1)} %get-tuple-element.24), channel_id=1, source_target_pairs={{0,4},{4,0},{1,5},{5,1},{2,6},{6,2},{3,7},{7,3},{8,12},{12,8},{9,1... | collective-permute-start | bytes 393224 | tf_op jit(solution)/shard_map/ppermute | solution.py:90
  58.4 1.6 %collective-permute-start.21 = (f32[32,1024]{1,0:T(8,128)S(1)}, f32[32,1024]{1,0:T(8,128)S(1)}, u32[]{:S(2)}, u32[]{:S(2)}) collective-permute-start(f32[32,1024]{1,0:T(8,128)S(1)} %get-tuple-element.24), channel_id=1, source_target_pairs={{0,16},{8,24},{16,0},{24,8},{1,17},{9,25},{17,1},{25,9},{2,18},{10... | collective-permute-start | bytes 393224 | tf_op jit(solution)/shard_map/ppermute | solution.py:93
  60.1 2.2 %collective-permute-done.13 = f32[32,1024]{1,0:T(8,128)S(1)} collective-permute-done((f32[32,1024]{1,0:T(8,128)S(1)}, f32[32,1024]{1,0:T(8,128)S(1)}, u32[]{:S(2)}, u32[]{:S(2)}) %collective-permute-start.13) | collective-permute-done | bytes 131104 | tf_op jit(solution)/shard_map/ppermute | solution.py:93
  62.2 1.8 %collective-permute-start.28 = (f32[32,1024]{1,0:T(8,128)S(1)}, f32[32,1024]{1,0:T(8,128)S(1)}, u32[]{:S(2)}, u32[]{:S(2)}) collective-permute-start(f32[32,1024]{1,0:T(8,128)S(1)} %get-tuple-element.29), channel_id=1, source_target_pairs={{0,4},{4,0},{1,5},{5,1},{2,6},{6,2},{3,7},{7,3},{8,12},{12,8},{9,1... | collective-permute-start | bytes 393224 | tf_op jit(solution)/shard_map/ppermute | solution.py:90
  64.5 2.1 %collective-permute-start.14 = (f32[32,1024]{1,0:T(8,128)S(1)}, f32[32,1024]{1,0:T(8,128)S(1)}, u32[]{:S(2)}, u32[]{:S(2)}) collective-permute-start(f32[32,1024]{1,0:T(8,128)S(1)} %get-tuple-element.67), channel_id=1, source_target_pairs={{0,4},{4,0},{8,24},{12,28},{16,20},{20,16},{24,8},{28,12},{1,5},{5... | collective-permute-start | bytes 393224 | tf_op jit(solution)/shard_map/ppermute | solution.py:107
  67.2 3.3 %collective-permute-done.29 = f32[32,1024]{1,0:T(8,128)S(1)} collective-permute-done((f32[32,1024]{1,0:T(8,128)S(1)}, f32[32,1024]{1,0:T(8,128)S(1)}, u32[]{:S(2)}, u32[]{:S(2)}) %collective-permute-start.29) | collective-permute-done | bytes 131104 | tf_op jit(solution)/shard_map/ppermute | solution.py:93
  72.2 3.3 %collective-permute-done.30 = f32[32,1024]{1,0:T(8,128)S(1)} collective-permute-done((f32[32,1024]{1,0:T(8,128)S(1)}, f32[32,1024]{1,0:T(8,128)S(1)}, u32[]{:S(2)}, u32[]{:S(2)}) %collective-permute-start.30) | collective-permute-done | bytes 131104 | tf_op jit(solution)/shard_map/ppermute | solution.py:107
  76.1 1.3 %collective-permute-done.31 = f32[32,3072]{1,0:T(8,128)S(1)} collective-permute-done((f32[32,3072]{1,0:T(8,128)S(1)}, f32[32,3072]{1,0:T(8,128)S(1)}, u32[]{:S(2)}, u32[]{:S(2)}) %collective-permute-start.31) | collective-permute-done | bytes 393248 | tf_op jit(solution)/shard_map/ppermute | solution.py:110
  77.5 2.4 %pad_maximum_fusion = f32[128,8192]{1,0:T(8,128)} fusion(f32[32,8192]{1,0:T(8,128)S(1)} %slice_dynamic-update-slice_fusion, f32[32,8192]{1,0:T(8,128)S(1)} %slice_dynamic-update-slice_fusion.3, f32[32,8192]{1,0:T(8,128)S(1)} %slice_dynamic-update-slice_fusion.6, f32[32,8192]{1,0:T(8,128)S(1)} %slice_dynamic-update-slice_fusion.9), kind=kLoop, calls=%fused_computation | loop fusion | flops 3145728 | bytes 8388608 | tf_op jit(solution)/shard_map/concatenate | solution.py:139
  (112 shorter events, 10.7 us)
Async XLA Ops:
  2.3 23.4 %collective-permute-start = (bf16[32,4096]{1,0:T(8,128)(2,1)S(1)}, bf16[32,4096]{1,0:T(8,128)(2,1)S(1)}, u32[]{:S(2)}, u32[]{:S(2)}) collective-permute-start(bf16[32,4096]{1,0:T(8,128)(2,1)S(1)} %dynamic-slice_bitcast_fusion.3), channel_id=1, source_target_pairs={{0,4},{4,0},{1,5},{5,1},{2,6},{6,2},{3,7},{7,3},{8,12},{12,8},{9,1... | collective-permute-start | bytes 786440 | tf_op jit(solution)/shard_map/ppermute | solution.py:58
  5.4 20.4 %collective-permute-start.24 = (bf16[32,4096]{1,0:T(8,128)(2,1)S(1)}, bf16[32,4096]{1,0:T(8,128)(2,1)S(1)}, u32[]{:S(2)}, u32[]{:S(2)}) collective-permute-start(bf16[32,4096]{1,0:T(8,128)(2,1)S(1)} %dynamic-slice_bitcast_fusion), channel_id=1, source_target_pairs={{0,4},{4,0},{1,5},{5,1},{2,6},{6,2},{3,7},{7,3},{8,12},{12,8},{9,1... | collective-permute-start | bytes 786440 | tf_op jit(solution)/shard_map/ppermute | solution.py:58
  6.2 17.7 %collective-permute-start.16 = (bf16[32,4096]{1,0:T(8,128)(2,1)}, bf16[32,4096]{1,0:T(8,128)(2,1)}, u32[]{:S(2)}, u32[]{:S(2)}) collective-permute-start(bf16[32,4096]{1,0:T(8,128)(2,1)} %dynamic-slice_bitcast_fusion.1), channel_id=1, source_target_pairs={{0,4},{4,0},{1,5},{5,1},{2,6},{6,2},{3,7},{7,3},{8,12},{12,8},{9,1... | collective-permute-start | bytes 786440 | tf_op jit(solution)/shard_map/ppermute | solution.py:58
  8.9 19.6 %collective-permute-start.8 = (bf16[32,4096]{1,0:T(8,128)(2,1)}, bf16[32,4096]{1,0:T(8,128)(2,1)S(1)}, u32[]{:S(2)}, u32[]{:S(2)}) collective-permute-start(bf16[32,4096]{1,0:T(8,128)(2,1)} %dynamic-slice_bitcast_fusion.2), channel_id=1, source_target_pairs={{0,4},{4,0},{1,5},{5,1},{2,6},{6,2},{3,7},{7,3},{8,12},{12,8},{9,1... | collective-permute-start | bytes 786440 | tf_op jit(solution)/shard_map/ppermute | solution.py:58
  32.1 5.6 %collective-permute-start.25 = (f32[32,2048]{1,0:T(8,128)S(1)}, f32[32,2048]{1,0:T(8,128)S(1)}, u32[]{:S(2)}, u32[]{:S(2)}) collective-permute-start(f32[32,2048]{1,0:T(8,128)S(1)} %pad_maximum_fusion.8), channel_id=1, source_target_pairs={{0,8},{8,0},{16,24},{24,16},{1,9},{9,1},{17,25},{25,17},{2,10},{10... | collective-permute-start | bytes 786440 | tf_op jit(solution)/shard_map/ppermute | solution.py:70
  32.7 7.3 %collective-permute-start.9 = (f32[32,2048]{1,0:T(8,128)S(1)}, f32[32,2048]{1,0:T(8,128)S(1)}, u32[]{:S(2)}, u32[]{:S(2)}) collective-permute-start(f32[32,2048]{1,0:T(8,128)S(1)} %pad_maximum_fusion.6), channel_id=1, source_target_pairs={{0,8},{8,0},{16,24},{24,16},{1,9},{9,1},{17,25},{25,17},{2,10},{10... | collective-permute-start | bytes 786440 | tf_op jit(solution)/shard_map/ppermute | solution.py:70
  32.8 5.3 %collective-permute-start.1 = (f32[32,2048]{1,0:T(8,128)S(1)}, f32[32,2048]{1,0:T(8,128)S(1)}, u32[]{:S(2)}, u32[]{:S(2)}) collective-permute-start(f32[32,2048]{1,0:T(8,128)S(1)} %pad_maximum_fusion.5), channel_id=1, source_target_pairs={{0,8},{8,0},{16,24},{24,16},{1,9},{9,1},{17,25},{25,17},{2,10},{10... | collective-permute-start | bytes 786440 | tf_op jit(solution)/shard_map/ppermute | solution.py:70
  35.9 12.1 %collective-permute-start.18 = (f32[32,1024]{1,0:T(8,128)S(1)}, f32[32,1024]{1,0:T(8,128)S(1)}, u32[]{:S(2)}, u32[]{:S(2)}) collective-permute-start(f32[32,1024]{1,0:T(8,128)S(1)} %constant_dynamic-slice_fusion.5), channel_id=1, source_target_pairs={{0,16},{8,24},{16,0},{24,8},{1,17},{9,25},{17,1},{25,9},{2,18},{10... | collective-permute-start | bytes 393224 | tf_op jit(solution)/shard_map/ppermute | solution.py:74
  37.8 10.2 %collective-permute-start.26 = (f32[32,1024]{1,0:T(8,128)S(1)}, f32[32,1024]{1,0:T(8,128)S(1)}, u32[]{:S(2)}, u32[]{:S(2)}) collective-permute-start(f32[32,1024]{1,0:T(8,128)S(1)} %constant_dynamic-slice_fusion), channel_id=1, source_target_pairs={{0,16},{8,24},{16,0},{24,8},{1,17},{9,25},{17,1},{25,9},{2,18},{10... | collective-permute-start | bytes 393224 | tf_op jit(solution)/shard_map/ppermute | solution.py:74
  38.1 9.8 %collective-permute-start.2 = (f32[32,1024]{1,0:T(8,128)S(1)}, f32[32,1024]{1,0:T(8,128)S(1)}, u32[]{:S(2)}, u32[]{:S(2)}) collective-permute-start(f32[32,1024]{1,0:T(8,128)S(1)} %constant_dynamic-slice_fusion.15), channel_id=1, source_target_pairs={{0,16},{8,24},{16,0},{24,8},{1,17},{9,25},{17,1},{25,9},{2,18},{10... | collective-permute-start | bytes 393224 | tf_op jit(solution)/shard_map/ppermute | solution.py:74
  40.0 9.8 %collective-permute-start.10 = (f32[32,1024]{1,0:T(8,128)S(1)}, f32[32,1024]{1,0:T(8,128)S(1)}, u32[]{:S(2)}, u32[]{:S(2)}) collective-permute-start(f32[32,1024]{1,0:T(8,128)S(1)} %constant_dynamic-slice_fusion.10), channel_id=1, source_target_pairs={{0,16},{8,24},{16,0},{24,8},{1,17},{9,25},{17,1},{25,9},{2,18},{10... | collective-permute-start | bytes 393224 | tf_op jit(solution)/shard_map/ppermute | solution.py:74
  50.1 6.1 %collective-permute-start.3 = (f32[32,1024]{1,0:T(8,128)S(1)}, f32[32,1024]{1,0:T(8,128)S(1)}, u32[]{:S(2)}, u32[]{:S(2)}) collective-permute-start(f32[32,1024]{1,0:T(8,128)S(1)} %get-tuple-element.14), channel_id=1, source_target_pairs={{0,8},{8,0},{16,24},{24,16},{1,9},{9,1},{17,25},{25,17},{2,10},{10... | collective-permute-start | bytes 393224 | tf_op jit(solution)/shard_map/ppermute | solution.py:87
  50.2 6.3 %collective-permute-start.4 = (f32[32,1024]{1,0:T(8,128)S(1)}, f32[32,1024]{1,0:T(8,128)S(1)}, u32[]{:S(2)}, u32[]{:S(2)}) collective-permute-start(f32[32,1024]{1,0:T(8,128)S(1)} %get-tuple-element.14), channel_id=1, source_target_pairs={{0,4},{4,0},{1,5},{5,1},{2,6},{6,2},{3,7},{7,3},{8,12},{12,8},{9,1... | collective-permute-start | bytes 393224 | tf_op jit(solution)/shard_map/ppermute | solution.py:90
  51.9 5.6 %collective-permute-start.5 = (f32[32,1024]{1,0:T(8,128)S(1)}, f32[32,1024]{1,0:T(8,128)S(1)}, u32[]{:S(2)}, u32[]{:S(2)}) collective-permute-start(f32[32,1024]{1,0:T(8,128)S(1)} %get-tuple-element.14), channel_id=1, source_target_pairs={{0,16},{8,24},{16,0},{24,8},{1,17},{9,25},{17,1},{25,9},{2,18},{10... | collective-permute-start | bytes 393224 | tf_op jit(solution)/shard_map/ppermute | solution.py:93
  53.7 6.3 %collective-permute-start.12 = (f32[32,1024]{1,0:T(8,128)S(1)}, f32[32,1024]{1,0:T(8,128)S(1)}, u32[]{:S(2)}, u32[]{:S(2)}) collective-permute-start(f32[32,1024]{1,0:T(8,128)S(1)} %get-tuple-element.19), channel_id=1, source_target_pairs={{0,4},{4,0},{1,5},{5,1},{2,6},{6,2},{3,7},{7,3},{8,12},{12,8},{9,1... | collective-permute-start | bytes 393224 | tf_op jit(solution)/shard_map/ppermute | solution.py:90
  56.2 6.1 %collective-permute-start.13 = (f32[32,1024]{1,0:T(8,128)S(1)}, f32[32,1024]{1,0:T(8,128)S(1)}, u32[]{:S(2)}, u32[]{:S(2)}) collective-permute-start(f32[32,1024]{1,0:T(8,128)S(1)} %get-tuple-element.19), channel_id=1, source_target_pairs={{0,16},{8,24},{16,0},{24,8},{1,17},{9,25},{17,1},{25,9},{2,18},{10... | collective-permute-start | bytes 393224 | tf_op jit(solution)/shard_map/ppermute | solution.py:93
  56.5 7.6 %collective-permute-start.19 = (f32[32,1024]{1,0:T(8,128)S(1)}, f32[32,1024]{1,0:T(8,128)S(1)}, u32[]{:S(2)}, u32[]{:S(2)}) collective-permute-start(f32[32,1024]{1,0:T(8,128)S(1)} %get-tuple-element.24), channel_id=1, source_target_pairs={{0,8},{8,0},{16,24},{24,16},{1,9},{9,1},{17,25},{25,17},{2,10},{10... | collective-permute-start | bytes 393224 | tf_op jit(solution)/shard_map/ppermute | solution.py:87
  57.5 6.8 %collective-permute-start.20 = (f32[32,1024]{1,0:T(8,128)S(1)}, f32[32,1024]{1,0:T(8,128)S(1)}, u32[]{:S(2)}, u32[]{:S(2)}) collective-permute-start(f32[32,1024]{1,0:T(8,128)S(1)} %get-tuple-element.24), channel_id=1, source_target_pairs={{0,4},{4,0},{1,5},{5,1},{2,6},{6,2},{3,7},{7,3},{8,12},{12,8},{9,1... | collective-permute-start | bytes 393224 | tf_op jit(solution)/shard_map/ppermute | solution.py:90
  58.4 6.1 %collective-permute-start.21 = (f32[32,1024]{1,0:T(8,128)S(1)}, f32[32,1024]{1,0:T(8,128)S(1)}, u32[]{:S(2)}, u32[]{:S(2)}) collective-permute-start(f32[32,1024]{1,0:T(8,128)S(1)} %get-tuple-element.24), channel_id=1, source_target_pairs={{0,16},{8,24},{16,0},{24,8},{1,17},{9,25},{17,1},{25,9},{2,18},{10... | collective-permute-start | bytes 393224 | tf_op jit(solution)/shard_map/ppermute | solution.py:93
  60.0 6.6 %collective-permute-start.27 = (f32[32,1024]{1,0:T(8,128)S(1)}, f32[32,1024]{1,0:T(8,128)S(1)}, u32[]{:S(2)}, u32[]{:S(2)}) collective-permute-start(f32[32,1024]{1,0:T(8,128)S(1)} %get-tuple-element.29), channel_id=1, source_target_pairs={{0,8},{8,0},{16,24},{24,16},{1,9},{9,1},{17,25},{25,17},{2,10},{10... | collective-permute-start | bytes 393224 | tf_op jit(solution)/shard_map/ppermute | solution.py:87
  64.1 6.4 %collective-permute-start.29 = (f32[32,1024]{1,0:T(8,128)S(1)}, f32[32,1024]{1,0:T(8,128)S(1)}, u32[]{:S(2)}, u32[]{:S(2)}) collective-permute-start(f32[32,1024]{1,0:T(8,128)S(1)} %get-tuple-element.29), channel_id=1, source_target_pairs={{0,16},{8,24},{16,0},{24,8},{1,17},{9,25},{17,1},{25,9},{2,18},{10... | collective-permute-start | bytes 393224 | tf_op jit(solution)/shard_map/ppermute | solution.py:93
  64.3 6.6 %collective-permute-start.6 = (f32[32,1024]{1,0:T(8,128)S(1)}, f32[32,1024]{1,0:T(8,128)S(1)}, u32[]{:S(2)}, u32[]{:S(2)}) collective-permute-start(f32[32,1024]{1,0:T(8,128)S(1)} %get-tuple-element.65), channel_id=1, source_target_pairs={{0,4},{4,0},{8,24},{12,28},{16,20},{20,16},{24,8},{28,12},{1,5},{5... | collective-permute-start | bytes 393224 | tf_op jit(solution)/shard_map/ppermute | solution.py:107
  64.5 6.4 %collective-permute-start.14 = (f32[32,1024]{1,0:T(8,128)S(1)}, f32[32,1024]{1,0:T(8,128)S(1)}, u32[]{:S(2)}, u32[]{:S(2)}) collective-permute-start(f32[32,1024]{1,0:T(8,128)S(1)} %get-tuple-element.67), channel_id=1, source_target_pairs={{0,4},{4,0},{8,24},{12,28},{16,20},{20,16},{24,8},{28,12},{1,5},{5... | collective-permute-start | bytes 393224 | tf_op jit(solution)/shard_map/ppermute | solution.py:107
  66.6 5.5 %collective-permute-start.22 = (f32[32,1024]{1,0:T(8,128)S(1)}, f32[32,1024]{1,0:T(8,128)S(1)}, u32[]{:S(2)}, u32[]{:S(2)}) collective-permute-start(f32[32,1024]{1,0:T(8,128)S(1)} %get-tuple-element.69), channel_id=1, source_target_pairs={{0,4},{4,0},{8,24},{12,28},{16,20},{20,16},{24,8},{28,12},{1,5},{5... | collective-permute-start | bytes 393224 | tf_op jit(solution)/shard_map/ppermute | solution.py:107
  (11 other events, 77.7 us)

commit v3 on v2

--- a/solution.py
+++ b/solution.py
@@ -117,17 +117,24 @@
     return out
 
 
-CHUNKS = 4
+CHUNK_WEIGHTS = (2, 4, 5, 5)
+
+
+def chunk_rows(row_count):
+    unit = row_count // sum(CHUNK_WEIGHTS)
+    if unit % 8 or unit * sum(CHUNK_WEIGHTS) != row_count:
+        return [row_count // 4] * 4
+    return [unit * w for w in CHUNK_WEIGHTS]
 
 
 def local(grad_parts, inner_params, first_moment, second_moment, outer_params, outer_momentum):
     replicas = lax.axis_size("replica")
     share_cols = outer_params.shape[2]
-    row_count = inner_params.shape[1]
-    chunk = row_count // CHUNKS
     pieces = []
-    for index in range(CHUNKS):
-        rows = slice(index * chunk, (index + 1) * chunk)
+    begin = 0
+    for size in chunk_rows(inner_params.shape[1]):
+        rows = slice(begin, begin + size)
+        begin += size
         gradient = fsdp_sum(grad_parts[0, 0, rows])
         first_out, second_out, updated = inner_adamw(
             gradient, inner_params[0, rows], first_moment[0, rows], second_moment[0, rows]

time: 80.1 us -> 77.1 us (0.963)
  waiting for transfers between devices: 39.2 us -> 28.7 us
  local copies, waits for them, and re-layouts: 4.1 us -> 7.95 us
  other arithmetic: 12.3 us -> 15.1 us
  starting transfers between devices: 23 us -> 23.9 us
    ppermute x4, waiting for transfers between devices: 17.7 us -> 6.07 us  [fsdp_sum(): got = lax.ppermute(send, 'fsdp', shifted(fsdp_count, step))]
    ppermute x4, waiting for transfers between devices: 6.42 us -> 3.25 us  [gather_weights(): lax.ppermute(share, 'replica', shifted(replicas, step, stride=2))]
    slice x1 -> x3, local copies, waits for them, and re-layouts: 1.65 us -> 3.56 us  [local(): gradient = fsdp_sum(grad_parts[0, 0, rows])]
    ppermute x4, waiting for transfers between devices: 3.91 us -> 5.57 us  [gather_weights(): got = lax.ppermute(payload, ('replica', 'fsdp'), routes)]
    ppermute x4, waiting for transfers between devices: 0.5 us -> 1.91 us  [gather_weights(): along_x[step] = lax.ppermute(share, 'fsdp', shifted(fsdp_count, step))]
    ppermute x4, starting transfers between devices: 2.66 us -> 3.94 us  [gather_weights(): got = lax.ppermute(payload, ('replica', 'fsdp'), routes)]
    sub x2 -> x3, other arithmetic: 5.07 us -> 6.32 us  [inner_adamw(): updated = params - inner_rate * (direction + weight_decay * params)]
    ppermute x4, starting transfers between devices: 4.31 us -> 5.42 us  [replica_sum(): lax.ppermute(send, 'replica', shifted(replicas, step, stride=2))]
  transfers between devices with their start and end apart: 32 -> 32, of which waited for: 11 -> 13; matrix products, arithmetic and copies ran while one was open for 11% -> 24% of each run, Pallas kernels for 0% -> 0%
where the time goes in v3:
time: 77.1 us; the launch traced here: 76.8 us
  waiting for transfers between devices  28.7 us (37%)
  starting transfers between devices  23.9 us (31%)
  other arithmetic  15.1 us (20%)
  local copies, waits for them, and re-layouts  7.95 us (10%)
  between operations  1.25 us (2%)
    ppermute x4, waiting for transfers between devices, replica_sum(): lax.ppermute(send, 'replica', shifted(replicas, step, stride=2))  9.54 us
    sub x3, other arithmetic, inner_adamw(): updated = params - inner_rate * (direction + weight_decay * params)  6.32 us
    ppermute x4, waiting for transfers between devices, fsdp_sum(): got = lax.ppermute(send, 'fsdp', shifted(fsdp_count, step))  6.07 us
    ppermute x4, waiting for transfers between devices, gather_weights(): got = lax.ppermute(payload, ('replica', 'fsdp'), routes)  5.57 us
    ppermute x4, starting transfers between devices, replica_sum(): lax.ppermute(send, 'replica', shifted(replicas, step, stride=2))  5.42 us
    ppermute x4, starting transfers between devices, fsdp_sum(): got = lax.ppermute(send, 'fsdp', shifted(fsdp_count, step))  5.08 us
    ppermute x4, starting transfers between devices, gather_weights(): along_x[step] = lax.ppermute(share, 'fsdp', shifted(fsdp_count, step))  4.46 us
    ppermute x4, starting transfers between devices, gather_weights(): got = lax.ppermute(payload, ('replica', 'fsdp'), routes)  3.94 us
  transfers between devices with their start and end apart: 32, of which 13 were waited for; matrix products, arithmetic and copies ran while one was open for 24% of the time, Pallas kernels for 0%

profile of v3, /device:TPU:0, one launch (start us, length us, event | category | flops | bytes accessed | tf_op | source)
XLA Modules:
  0.0 76.8 jit_solution(17133057541900539976)
XLA Ops:
  1.7 3.0 %collective-permute-start = (bf16[16,4096]{1,0:T(8,128)(2,1)S(1)}, bf16[16,4096]{1,0:T(8,128)(2,1)}, u32[]{:S(2)}, u32[]{:S(2)}) collective-permute-start(bf16[16,4096]{1,0:T(8,128)(2,1)S(1)} %dynamic-slice_bitcast_fusion.3), channel_id=1, source_target_pairs={{0,4},{4,0},{1,5},{5,1},{2,6},{6,2},{3,7},{7,3},{8,12},{12,8},{9,1... | collective-permute-start | bytes 393224 | tf_op jit(solution)/shard_map/ppermute | solution.py:58
  6.7 1.5 %fusion.16 = (bf16[1,1,40,8192]{3,2,1,0:T(8,128)(2,1)S(1)}, bf16[1,1,40,8192]{3,2,1,0:T(8,128)(2,1)S(1)}) fusion(bf16[1,1,128,8192]{3,2,1,0:T(8,128)(2,1)} %param.6), kind=kLoop, calls=%fused_computation.121 | loop fusion | bytes 2621440 | tf_op jit(solution)/shard_map/slice | solution.py:138
  9.0 1.9 %collective-permute-start.24 = (bf16[40,4096]{1,0:T(8,128)(2,1)}, bf16[40,4096]{1,0:T(8,128)(2,1)}, u32[]{:S(2)}, u32[]{:S(2)}) collective-permute-start(bf16[40,4096]{1,0:T(8,128)(2,1)} %dynamic-slice_bitcast_fusion), channel_id=1, source_target_pairs={{0,4},{4,0},{1,5},{5,1},{2,6},{6,2},{3,7},{7,3},{8,12},{12,8},{9,1... | collective-permute-start | bytes 983048 | tf_op jit(solution)/shard_map/ppermute | solution.py:58
  10.8 2.2 %bitcast_subtract_fusion.3 = (f32[16,4096]{1,0:T(8,128)S(1)}, f32[16,4096]{1,0:T(8,128)}, f32[16,4096]{1,0:T(8,128)}) fusion(f32[1,128,4096]{2,1,0:T(8,128)S(1)} %copy-done, bf16[16,4096]{1,0:T(8,128)(2,1)} %collective-permute-done, bf16[1,1,16,8192]{3,2,1,0:T(8,128)(2,1)} %copy-done.8, s32[]{:T(128)S(6)} %select_n.208, f32[1,128,4096]{2,1,0:T(8,128)} %param.8, ...), kind=kLoop, calls=%fused_computation.44 | loop fusion | flops 1179648 | bytes 1835012 | tf_op jit(solution)/shard_map/sub | solution.py:24
  16.3 1.6 %collective-permute-start.2 = (f32[16,1024]{1,0:T(8,128)S(1)}, f32[16,1024]{1,0:T(8,128)S(1)}, u32[]{:S(2)}, u32[]{:S(2)}) collective-permute-start(f32[16,1024]{1,0:T(8,128)S(1)} %constant_dynamic-slice_fusion.15), channel_id=1, source_target_pairs={{0,16},{8,24},{16,0},{24,8},{1,17},{9,25},{17,1},{25,9},{2,18},{10... | collective-permute-start | bytes 196616 | tf_op jit(solution)/shard_map/ppermute | solution.py:74
  17.9 2.0 %bitcast_subtract_fusion.2 = (f32[32,4096]{1,0:T(8,128)S(1)}, f32[32,4096]{1,0:T(8,128)S(1)}, f32[32,4096]{1,0:T(8,128)S(1)}) fusion(f32[1,128,4096]{2,1,0:T(8,128)S(1)} %copy-done, bf16[32,4096]{1,0:T(8,128)(2,1)} %collective-permute-done.8, bf16[1,1,32,8192]{3,2,1,0:T(8,128)(2,1)} %copy-done.5, s32[]{:T(128)S(6)} %select_n.208, f32[1,128,4096]{2,1,0:T(8,128)} %param.8, ...), kind=kLoop, calls=%fused_computation.25 | loop fusion | flops 2359296 | bytes 3670020 | tf_op jit(solution)/shard_map/sub | solution.py:24
  21.0 1.3 %collective-permute-start.5 = (f32[16,1024]{1,0:T(8,128)S(1)}, f32[16,1024]{1,0:T(8,128)S(1)}, u32[]{:S(2)}, u32[]{:S(2)}) collective-permute-start(f32[16,1024]{1,0:T(8,128)S(1)} %get-tuple-element.14), channel_id=1, source_target_pairs={{0,16},{8,24},{16,0},{24,8},{1,17},{9,25},{17,1},{25,9},{2,18},{10... | collective-permute-start | bytes 196616 | tf_op jit(solution)/shard_map/ppermute | solution.py:93
  23.4 6.1 %collective-permute-done.16 = bf16[40,4096]{1,0:T(8,128)(2,1)} collective-permute-done((bf16[40,4096]{1,0:T(8,128)(2,1)}, bf16[40,4096]{1,0:T(8,128)(2,1)}, u32[]{:S(2)}, u32[]{:S(2)}) %collective-permute-start.16) | collective-permute-done | bytes 327712 | tf_op jit(solution)/shard_map/ppermute | solution.py:58
  29.5 2.2 %bitcast_subtract_fusion.1 = (f32[40,4096]{1,0:T(8,128)S(1)}, f32[40,4096]{1,0:T(8,128)S(1)}, f32[40,4096]{1,0:T(8,128)S(1)}, f32[40,4096]{1,0:T(8,128)S(1)}, f32[40,4096]{1,0:T(8,128)S(1)}, /*index=5*/f32[40,4096]{1,0:T(8,128)S(1)}) fusion(f32[1,128,4096]{2,1,0:T(8,128)S(1)} %copy-done, bf16[40,4096]{1,0:T(8,128)(2,1)} %collective-permute-done.16, ...), kind=kLoop, calls=%fused_computation.16 | loop fusion | flops 5898240 | bytes 9175044 | tf_op jit(solution)/shard_map/sub | solution.py:24
  32.7 2.4 %maximum_bitcast_fusion = (f32[1,128,4096]{2,1,0:T(8,128)}, f32[1,128,4096]{2,1,0:T(8,128)}) fusion(f32[40,4096]{1,0:T(8,128)S(1)} %get-tuple-element.35, f32[40,4096]{1,0:T(8,128)S(1)} %get-tuple-element.26, f32[32,4096]{1,0:T(8,128)S(1)} %get-tuple-element.21, f32[16,4096]{1,0:T(8,128)S(1)} %copy-done.6, f32[40,4096]{1,0:T(8,128)S(1)} %get-tuple-element.34, ...), kind=kLoop, calls=%fused_computation.1 | loop fusion | flops 3145728 | bytes 8388608 | tf_op jit(solution)/shard_map/broadcast_in_dim | solution.py:148
  36.3 1.7 %collective-permute-start.10 = (f32[32,1024]{1,0:T(8,128)S(1)}, f32[32,1024]{1,0:T(8,128)S(1)}, u32[]{:S(2)}, u32[]{:S(2)}) collective-permute-start(f32[32,1024]{1,0:T(8,128)S(1)} %constant_dynamic-slice_fusion.10), channel_id=1, source_target_pairs={{0,16},{8,24},{16,0},{24,8},{1,17},{9,25},{17,1},{25,9},{2,18},{10... | collective-permute-start | bytes 393224 | tf_op jit(solution)/shard_map/ppermute | solution.py:74
  38.0 1.7 %collective-permute-done.6 = f32[16,1024]{1,0:T(8,128)S(1)} collective-permute-done((f32[16,1024]{1,0:T(8,128)S(1)}, f32[16,1024]{1,0:T(8,128)S(1)}, u32[]{:S(2)}, u32[]{:S(2)}) %collective-permute-start.6) | collective-permute-done | bytes 65568 | tf_op jit(solution)/shard_map/ppermute | solution.py:107
  39.8 2.9 %collective-permute-done.10 = f32[32,1024]{1,0:T(8,128)S(1)} collective-permute-done((f32[32,1024]{1,0:T(8,128)S(1)}, f32[32,1024]{1,0:T(8,128)S(1)}, u32[]{:S(2)}, u32[]{:S(2)}) %collective-permute-start.10) | collective-permute-done | bytes 131104 | tf_op jit(solution)/shard_map/ppermute | solution.py:74
  44.7 1.2 %collective-permute-start.18 = (f32[40,1024]{1,0:T(8,128)S(1)}, f32[40,1024]{1,0:T(8,128)S(1)}, u32[]{:S(2)}, u32[]{:S(2)}) collective-permute-start(f32[40,1024]{1,0:T(8,128)S(1)} %constant_dynamic-slice_fusion.5), channel_id=1, source_target_pairs={{0,16},{8,24},{16,0},{24,8},{1,17},{9,25},{17,1},{25,9},{2,18},{10... | collective-permute-start | bytes 491528 | tf_op jit(solution)/shard_map/ppermute | solution.py:74
  47.1 1.7 %collective-permute-done.13 = f32[32,1024]{1,0:T(8,128)S(1)} collective-permute-done((f32[32,1024]{1,0:T(8,128)S(1)}, f32[32,1024]{1,0:T(8,128)S(1)}, u32[]{:S(2)}, u32[]{:S(2)}) %collective-permute-start.13) | collective-permute-done | bytes 131104 | tf_op jit(solution)/shard_map/ppermute | solution.py:93
  49.7 2.6 %collective-permute-done.18 = f32[40,1024]{1,0:T(8,128)S(1)} collective-permute-done((f32[40,1024]{1,0:T(8,128)S(1)}, f32[40,1024]{1,0:T(8,128)S(1)}, u32[]{:S(2)}, u32[]{:S(2)}) %collective-permute-start.18) | collective-permute-done | bytes 163872 | tf_op jit(solution)/shard_map/ppermute | solution.py:74
  52.4 3.5 %collective-permute-done.26 = f32[40,1024]{1,0:T(8,128)S(1)} collective-permute-done((f32[40,1024]{1,0:T(8,128)S(1)}, f32[40,1024]{1,0:T(8,128)S(1)}, u32[]{:S(2)}, u32[]{:S(2)}) %collective-permute-start.26) | collective-permute-done | bytes 163872 | tf_op jit(solution)/shard_map/ppermute | solution.py:74
  60.7 1.3 %collective-permute-start.20 = (f32[40,1024]{1,0:T(8,128)S(1)}, f32[40,1024]{1,0:T(8,128)S(1)}, u32[]{:S(2)}, u32[]{:S(2)}) collective-permute-start(f32[40,1024]{1,0:T(8,128)S(1)} %get-tuple-element.24), channel_id=1, source_target_pairs={{0,4},{4,0},{1,5},{5,1},{2,6},{6,2},{3,7},{7,3},{8,12},{12,8},{9,1... | collective-permute-start | bytes 491528 | tf_op jit(solution)/shard_map/ppermute | solution.py:90
  63.5 1.5 %collective-permute-done.21 = f32[40,1024]{1,0:T(8,128)S(1)} collective-permute-done((f32[40,1024]{1,0:T(8,128)S(1)}, f32[40,1024]{1,0:T(8,128)S(1)}, u32[]{:S(2)}, u32[]{:S(2)}) %collective-permute-start.21) | collective-permute-done | bytes 163872 | tf_op jit(solution)/shard_map/ppermute | solution.py:93
  65.1 1.9 %collective-permute-done.20 = f32[40,1024]{1,0:T(8,128)S(1)} collective-permute-done((f32[40,1024]{1,0:T(8,128)S(1)}, f32[40,1024]{1,0:T(8,128)S(1)}, u32[]{:S(2)}, u32[]{:S(2)}) %collective-permute-start.20) | collective-permute-done | bytes 163872 | tf_op jit(solution)/shard_map/ppermute | solution.py:90
  67.0 1.4 %collective-permute-start.22 = (f32[40,1024]{1,0:T(8,128)S(1)}, f32[40,1024]{1,0:T(8,128)S(1)}, u32[]{:S(2)}, u32[]{:S(2)}) collective-permute-start(f32[40,1024]{1,0:T(8,128)S(1)} %get-tuple-element.56), channel_id=1, source_target_pairs={{0,4},{4,0},{8,24},{12,28},{16,20},{20,16},{24,8},{28,12},{1,5},{5... | collective-permute-start | bytes 491528 | tf_op jit(solution)/shard_map/ppermute | solution.py:107
  68.9 3.5 %collective-permute-done.22 = f32[40,1024]{1,0:T(8,128)S(1)} collective-permute-done((f32[40,1024]{1,0:T(8,128)S(1)}, f32[40,1024]{1,0:T(8,128)S(1)}, u32[]{:S(2)}, u32[]{:S(2)}) %collective-permute-start.22) | collective-permute-done | bytes 163872 | tf_op jit(solution)/shard_map/ppermute | solution.py:107
  72.8 1.6 %collective-permute-done.23 = f32[40,3072]{1,0:T(8,128)S(1)} collective-permute-done((f32[40,3072]{1,0:T(8,128)S(1)}, f32[40,3072]{1,0:T(8,128)S(1)}, u32[]{:S(2)}, u32[]{:S(2)}) %collective-permute-start.23) | collective-permute-done | bytes 491552 | tf_op jit(solution)/shard_map/ppermute | solution.py:110
  74.5 2.3 %pad_maximum_fusion = f32[128,8192]{1,0:T(8,128)} fusion(f32[40,8192]{1,0:T(8,128)S(1)} %slice_dynamic-update-slice_fusion, f32[40,8192]{1,0:T(8,128)S(1)} %slice_dynamic-update-slice_fusion.3, f32[32,8192]{1,0:T(8,128)S(1)} %slice_dynamic-update-slice_fusion.6, f32[16,8192]{1,0:T(8,128)S(1)} %slice_dynamic-update-slice_fusion.9), kind=kLoop, calls=%fused_computation | loop fusion | flops 3145728 | bytes 8388608 | tf_op jit(solution)/shard_map/concatenate | solution.py:146
  (130 shorter events, 22.5 us)
Async XLA Ops:
  1.7 9.2 %collective-permute-start = (bf16[16,4096]{1,0:T(8,128)(2,1)S(1)}, bf16[16,4096]{1,0:T(8,128)(2,1)}, u32[]{:S(2)}, u32[]{:S(2)}) collective-permute-start(bf16[16,4096]{1,0:T(8,128)(2,1)S(1)} %dynamic-slice_bitcast_fusion.3), channel_id=1, source_target_pairs={{0,4},{4,0},{1,5},{5,1},{2,6},{6,2},{3,7},{7,3},{8,12},{12,8},{9,1... | collective-permute-start | bytes 393224 | tf_op jit(solution)/shard_map/ppermute | solution.py:58
  6.7 11.2 %collective-permute-start.8 = (bf16[32,4096]{1,0:T(8,128)(2,1)}, bf16[32,4096]{1,0:T(8,128)(2,1)}, u32[]{:S(2)}, u32[]{:S(2)}) collective-permute-start(bf16[32,4096]{1,0:T(8,128)(2,1)} %dynamic-slice_bitcast_fusion.2), channel_id=1, source_target_pairs={{0,4},{4,0},{1,5},{5,1},{2,6},{6,2},{3,7},{7,3},{8,12},{12,8},{9,1... | collective-permute-start | bytes 786440 | tf_op jit(solution)/shard_map/ppermute | solution.py:58
  9.0 14.5 %collective-permute-start.24 = (bf16[40,4096]{1,0:T(8,128)(2,1)}, bf16[40,4096]{1,0:T(8,128)(2,1)}, u32[]{:S(2)}, u32[]{:S(2)}) collective-permute-start(bf16[40,4096]{1,0:T(8,128)(2,1)} %dynamic-slice_bitcast_fusion), channel_id=1, source_target_pairs={{0,4},{4,0},{1,5},{5,1},{2,6},{6,2},{3,7},{7,3},{8,12},{12,8},{9,1... | collective-permute-start | bytes 983048 | tf_op jit(solution)/shard_map/ppermute | solution.py:58
  14.4 15.1 %collective-permute-start.16 = (bf16[40,4096]{1,0:T(8,128)(2,1)}, bf16[40,4096]{1,0:T(8,128)(2,1)}, u32[]{:S(2)}, u32[]{:S(2)}) collective-permute-start(bf16[40,4096]{1,0:T(8,128)(2,1)} %dynamic-slice_bitcast_fusion.1), channel_id=1, source_target_pairs={{0,4},{4,0},{1,5},{5,1},{2,6},{6,2},{3,7},{7,3},{8,12},{12,8},{9,1... | collective-permute-start | bytes 983048 | tf_op jit(solution)/shard_map/ppermute | solution.py:58
  20.0 16.2 %collective-permute-start.9 = (f32[32,2048]{1,0:T(8,128)S(1)}, f32[32,2048]{1,0:T(8,128)S(1)}, u32[]{:S(2)}, u32[]{:S(2)}) collective-permute-start(f32[32,2048]{1,0:T(8,128)S(1)} %pad_maximum_fusion.6), channel_id=1, source_target_pairs={{0,8},{8,0},{16,24},{24,16},{1,9},{9,1},{17,25},{25,17},{2,10},{10... | collective-permute-start | bytes 786440 | tf_op jit(solution)/shard_map/ppermute | solution.py:70
  21.0 14.3 %collective-permute-start.5 = (f32[16,1024]{1,0:T(8,128)S(1)}, f32[16,1024]{1,0:T(8,128)S(1)}, u32[]{:S(2)}, u32[]{:S(2)}) collective-permute-start(f32[16,1024]{1,0:T(8,128)S(1)} %get-tuple-element.14), channel_id=1, source_target_pairs={{0,16},{8,24},{16,0},{24,8},{1,17},{9,25},{17,1},{25,9},{2,18},{10... | collective-permute-start | bytes 196616 | tf_op jit(solution)/shard_map/ppermute | solution.py:93
  22.3 13.0 %collective-permute-start.4 = (f32[16,1024]{1,0:T(8,128)S(1)}, f32[16,1024]{1,0:T(8,128)S(1)}, u32[]{:S(2)}, u32[]{:S(2)}) collective-permute-start(f32[16,1024]{1,0:T(8,128)S(1)} %get-tuple-element.14), channel_id=1, source_target_pairs={{0,4},{4,0},{1,5},{5,1},{2,6},{6,2},{3,7},{7,3},{8,12},{12,8},{9,1... | collective-permute-start | bytes 196616 | tf_op jit(solution)/shard_map/ppermute | solution.py:90
  23.4 11.8 %collective-permute-start.3 = (f32[16,1024]{1,0:T(8,128)S(1)}, f32[16,1024]{1,0:T(8,128)S(1)}, u32[]{:S(2)}, u32[]{:S(2)}) collective-permute-start(f32[16,1024]{1,0:T(8,128)S(1)} %get-tuple-element.14), channel_id=1, source_target_pairs={{0,8},{8,0},{16,24},{24,16},{1,9},{9,1},{17,25},{25,17},{2,10},{10... | collective-permute-start | bytes 196616 | tf_op jit(solution)/shard_map/ppermute | solution.py:87
  31.9 12.8 %collective-permute-start.17 = (f32[40,2048]{1,0:T(8,128)S(1)}, f32[40,2048]{1,0:T(8,128)S(1)}, u32[]{:S(2)}, u32[]{:S(2)}) collective-permute-start(f32[40,2048]{1,0:T(8,128)S(1)} %pad_maximum_fusion.4), channel_id=1, source_target_pairs={{0,8},{8,0},{16,24},{24,16},{1,9},{9,1},{17,25},{25,17},{2,10},{10... | collective-permute-start | bytes 983048 | tf_op jit(solution)/shard_map/ppermute | solution.py:70
  35.2 9.5 %collective-permute-start.25 = (f32[40,2048]{1,0:T(8,128)S(1)}, f32[40,2048]{1,0:T(8,128)S(1)}, u32[]{:S(2)}, u32[]{:S(2)}) collective-permute-start(f32[40,2048]{1,0:T(8,128)S(1)} %pad_maximum_fusion.5), channel_id=1, source_target_pairs={{0,8},{8,0},{16,24},{24,16},{1,9},{9,1},{17,25},{25,17},{2,10},{10... | collective-permute-start | bytes 983048 | tf_op jit(solution)/shard_map/ppermute | solution.py:70
  36.3 6.4 %collective-permute-start.10 = (f32[32,1024]{1,0:T(8,128)S(1)}, f32[32,1024]{1,0:T(8,128)S(1)}, u32[]{:S(2)}, u32[]{:S(2)}) collective-permute-start(f32[32,1024]{1,0:T(8,128)S(1)} %constant_dynamic-slice_fusion.10), channel_id=1, source_target_pairs={{0,16},{8,24},{16,0},{24,8},{1,17},{9,25},{17,1},{25,9},{2,18},{10... | collective-permute-start | bytes 393224 | tf_op jit(solution)/shard_map/ppermute | solution.py:74
  39.7 6.4 %collective-permute-start.7 = (f32[16,3072]{1,0:T(8,128)S(1)}, f32[16,3072]{1,0:T(8,128)S(1)}, u32[]{:S(2)}, u32[]{:S(2)}) collective-permute-start(f32[16,3072]{1,0:T(8,128)S(1)} %pad_maximum_fusion.7), channel_id=1, source_target_pairs={{0,8},{8,0},{16,24},{24,16},{1,9},{9,1},{17,25},{25,17},{2,10},{10... | collective-permute-start | bytes 589832 | tf_op jit(solution)/shard_map/ppermute | solution.py:110
  42.8 6.0 %collective-permute-start.13 = (f32[32,1024]{1,0:T(8,128)S(1)}, f32[32,1024]{1,0:T(8,128)S(1)}, u32[]{:S(2)}, u32[]{:S(2)}) collective-permute-start(f32[32,1024]{1,0:T(8,128)S(1)} %get-tuple-element.19), channel_id=1, source_target_pairs={{0,16},{8,24},{16,0},{24,8},{1,17},{9,25},{17,1},{25,9},{2,18},{10... | collective-permute-start | bytes 393224 | tf_op jit(solution)/shard_map/ppermute | solution.py:93
  43.8 5.1 %collective-permute-start.12 = (f32[32,1024]{1,0:T(8,128)S(1)}, f32[32,1024]{1,0:T(8,128)S(1)}, u32[]{:S(2)}, u32[]{:S(2)}) collective-permute-start(f32[32,1024]{1,0:T(8,128)S(1)} %get-tuple-element.19), channel_id=1, source_target_pairs={{0,4},{4,0},{1,5},{5,1},{2,6},{6,2},{3,7},{7,3},{8,12},{12,8},{9,1... | collective-permute-start | bytes 393224 | tf_op jit(solution)/shard_map/ppermute | solution.py:90
  44.7 7.6 %collective-permute-start.18 = (f32[40,1024]{1,0:T(8,128)S(1)}, f32[40,1024]{1,0:T(8,128)S(1)}, u32[]{:S(2)}, u32[]{:S(2)}) collective-permute-start(f32[40,1024]{1,0:T(8,128)S(1)} %constant_dynamic-slice_fusion.5), channel_id=1, source_target_pairs={{0,16},{8,24},{16,0},{24,8},{1,17},{9,25},{17,1},{25,9},{2,18},{10... | collective-permute-start | bytes 491528 | tf_op jit(solution)/shard_map/ppermute | solution.py:74
  46.1 9.8 %collective-permute-start.26 = (f32[40,1024]{1,0:T(8,128)S(1)}, f32[40,1024]{1,0:T(8,128)S(1)}, u32[]{:S(2)}, u32[]{:S(2)}) collective-permute-start(f32[40,1024]{1,0:T(8,128)S(1)} %constant_dynamic-slice_fusion), channel_id=1, source_target_pairs={{0,16},{8,24},{16,0},{24,8},{1,17},{9,25},{17,1},{25,9},{2,18},{10... | collective-permute-start | bytes 491528 | tf_op jit(solution)/shard_map/ppermute | solution.py:74
  48.8 11.8 %collective-permute-start.14 = (f32[32,1024]{1,0:T(8,128)S(1)}, f32[32,1024]{1,0:T(8,128)S(1)}, u32[]{:S(2)}, u32[]{:S(2)}) collective-permute-start(f32[32,1024]{1,0:T(8,128)S(1)} %get-tuple-element.60), channel_id=1, source_target_pairs={{0,4},{4,0},{8,24},{12,28},{16,20},{20,16},{24,8},{28,12},{1,5},{5... | collective-permute-start | bytes 393224 | tf_op jit(solution)/shard_map/ppermute | solution.py:107
  56.2 6.0 %collective-permute-start.29 = (f32[40,1024]{1,0:T(8,128)S(1)}, f32[40,1024]{1,0:T(8,128)S(1)}, u32[]{:S(2)}, u32[]{:S(2)}) collective-permute-start(f32[40,1024]{1,0:T(8,128)S(1)} %get-tuple-element.29), channel_id=1, source_target_pairs={{0,16},{8,24},{16,0},{24,8},{1,17},{9,25},{17,1},{25,9},{2,18},{10... | collective-permute-start | bytes 491528 | tf_op jit(solution)/shard_map/ppermute | solution.py:93
  57.0 5.7 %collective-permute-start.28 = (f32[40,1024]{1,0:T(8,128)S(1)}, f32[40,1024]{1,0:T(8,128)S(1)}, u32[]{:S(2)}, u32[]{:S(2)}) collective-permute-start(f32[40,1024]{1,0:T(8,128)S(1)} %get-tuple-element.29), channel_id=1, source_target_pairs={{0,4},{4,0},{1,5},{5,1},{2,6},{6,2},{3,7},{7,3},{8,12},{12,8},{9,1... | collective-permute-start | bytes 491528 | tf_op jit(solution)/shard_map/ppermute | solution.py:90
  58.1 7.0 %collective-permute-start.21 = (f32[40,1024]{1,0:T(8,128)S(1)}, f32[40,1024]{1,0:T(8,128)S(1)}, u32[]{:S(2)}, u32[]{:S(2)}) collective-permute-start(f32[40,1024]{1,0:T(8,128)S(1)} %get-tuple-element.24), channel_id=1, source_target_pairs={{0,16},{8,24},{16,0},{24,8},{1,17},{9,25},{17,1},{25,9},{2,18},{10... | collective-permute-start | bytes 491528 | tf_op jit(solution)/shard_map/ppermute | solution.py:93
  60.7 6.3 %collective-permute-start.20 = (f32[40,1024]{1,0:T(8,128)S(1)}, f32[40,1024]{1,0:T(8,128)S(1)}, u32[]{:S(2)}, u32[]{:S(2)}) collective-permute-start(f32[40,1024]{1,0:T(8,128)S(1)} %get-tuple-element.24), channel_id=1, source_target_pairs={{0,4},{4,0},{1,5},{5,1},{2,6},{6,2},{3,7},{7,3},{8,12},{12,8},{9,1... | collective-permute-start | bytes 491528 | tf_op jit(solution)/shard_map/ppermute | solution.py:90
  62.2 10.4 %collective-permute-start.15 = (f32[32,3072]{1,0:T(8,128)S(1)}, f32[32,3072]{1,0:T(8,128)S(1)}, u32[]{:S(2)}, u32[]{:S(2)}) collective-permute-start(f32[32,3072]{1,0:T(8,128)S(1)} %pad_maximum_fusion.3), channel_id=1, source_target_pairs={{0,8},{8,0},{16,24},{24,16},{1,9},{9,1},{17,25},{25,17},{2,10},{10... | collective-permute-start | bytes 1179656 | tf_op jit(solution)/shard_map/ppermute | solution.py:110
  62.7 6.0 %collective-permute-start.30 = (f32[40,1024]{1,0:T(8,128)S(1)}, f32[40,1024]{1,0:T(8,128)S(1)}, u32[]{:S(2)}, u32[]{:S(2)}) collective-permute-start(f32[40,1024]{1,0:T(8,128)S(1)} %get-tuple-element.58), channel_id=1, source_target_pairs={{0,4},{4,0},{8,24},{12,28},{16,20},{20,16},{24,8},{28,12},{1,5},{5... | collective-permute-start | bytes 491528 | tf_op jit(solution)/shard_map/ppermute | solution.py:107
  67.0 5.4 %collective-permute-start.22 = (f32[40,1024]{1,0:T(8,128)S(1)}, f32[40,1024]{1,0:T(8,128)S(1)}, u32[]{:S(2)}, u32[]{:S(2)}) collective-permute-start(f32[40,1024]{1,0:T(8,128)S(1)} %get-tuple-element.56), channel_id=1, source_target_pairs={{0,4},{4,0},{8,24},{12,28},{16,20},{20,16},{24,8},{28,12},{1,5},{5... | collective-permute-start | bytes 491528 | tf_op jit(solution)/shard_map/ppermute | solution.py:107
  (17 other events, 60.2 us)
